TPU v7x, 32 devices: a whole 2x2x4 slice. The times are simulated.
32 devices in a mesh: groups: 2 (over y), row: 8 (over z, x), col: 2 (over core).
Axes of the slice: x: 2, y: 2, z: 4, core: 2. Of those that a mesh axis runs over, the one named last changes fastest.
Arguments:
- feature_map: bfloat16 [256, 64, 256], P(('groups', 'row'), 'col'), parts along dimension 0, may hold values from -6 to 6
- cotangent: bfloat16 [256, 64, 256], P(('groups', 'row'), 'col'), parts along dimension 0, may hold values from -6 to 6
- kernel: float32 [49, 256], replicated, may hold values from -0.875 to 0.875
- kernel_bias: float32 [256], replicated, may hold values from -3 to 3
- norm_gain: float32 [256], replicated, may hold values from 0.25 to 1.75
- norm_bias: float32 [256], replicated, may hold values from -3 to 3
- weight_in: bfloat16 [256, 1024], replicated, may hold values from -0.375 to 0.375
- bias_in: float32 [1024], replicated, may hold values from -3 to 3
- weight_out: bfloat16 [1024, 256], replicated, may hold values from -0.1875 to 0.1875
- bias_out: float32 [256], replicated, may hold values from -3 to 3
- layer_scale: float32 [256], replicated, may hold values from 0.3 to 3
Outputs:
- grad_input: bfloat16 [256, 64, 256], P(('groups', 'row'), 'col'), parts along dimension 0
- grad_kernel: float32 [98, 256], P('groups'), parts along dimension 0
- grad_kernel_bias: float32 [512], P('groups'), parts along dimension 0
- grad_norm_gain: float32 [512], P('groups'), parts along dimension 0
- grad_norm_bias: float32 [512], P('groups'), parts along dimension 0
- grad_weight_in: float32 [512, 1024], P('groups'), parts along dimension 0
- grad_bias_in: float32 [2048], P('groups'), parts along dimension 0
- grad_weight_out: float32 [2048, 256], P('groups'), parts along dimension 0
- grad_bias_out: float32 [512], P('groups'), parts along dimension 0
- grad_layer_scale: float32 [512], P('groups'), parts along dimension 0
There are 2 independent parts, one for each index of `groups`. A program takes and returns all parts, laid end to end along the dimension named above; an argument that names none is the same for every part. Nothing has to cross between parts.
All inputs are finite; a program needn't handle non-finite values.
Results may differ from a plain program's by a relative error of at most 0.0065.
Values may be sent and summed in bfloat16 or wider, within the bound.
No kernel may reach another device: no remote copies, remote signals or barrier semaphores. Data moves between devices by JAX's collectives and lax.ppermute only.
A program may use at most 64 MiB of HBM per device.

v0:
```python
import jax
import jax.numpy as jnp
from jax import lax
from jax.sharding import PartitionSpec as P

KS = 7


def with_halo(block, sides, width):
    for axis, dim in sides:
        count = lax.axis_size(axis)
        forward = [(i, i + 1) for i in range(count - 1)]
        backward = [(target, source) for source, target in forward]
        low = lax.ppermute(
            lax.slice_in_dim(block, block.shape[dim] - width, None, axis=dim), axis, forward
        )
        high = lax.ppermute(lax.slice_in_dim(block, 0, width, axis=dim), axis, backward)
        block = jnp.concatenate([low, block, high], axis=dim)
    return block


def gelu_pair(pre_act):
    normal_cdf = 0.5 * (1.0 + lax.erf(pre_act * 0.7071067811865476))
    normal_pdf = jnp.exp(-0.5 * pre_act * pre_act) * 0.3989422804014327
    return (pre_act * normal_cdf, normal_cdf + pre_act * normal_pdf)


def depthwise(padded, kernel, row_count, col_count):
    running = jnp.zeros((row_count, col_count, kernel.shape[1]), jnp.float32)
    for tap_index in range(KS * KS):
        row_off, col_off = divmod(tap_index, KS)
        running = (
            running
            + padded[row_off : row_off + row_count, col_off : col_off + col_count]
            * kernel[tap_index]
        )
    return running


def forward_back(
    padded,
    grad_view,
    kernel,
    kernel_bias,
    norm_gain,
    norm_bias,
    weight_in,
    bias_in,
    weight_out,
    bias_out,
    layer_scale,
):
    row_count, col_count, channels = grad_view.shape
    contract_last = (((1,), (1,)), ((), ()))
    conv_out = depthwise(padded, kernel, row_count, col_count) + kernel_bias
    centred = conv_out - jnp.mean(conv_out, axis=2, keepdims=True)
    inv_std = lax.rsqrt(jnp.mean(centred * centred, axis=2, keepdims=True) + 1e-06)
    normed = centred * inv_std
    flat_in = (normed * norm_gain + norm_bias).astype(jnp.bfloat16).reshape(-1, channels)
    pre_act = jnp.dot(flat_in, weight_in, preferred_element_type=jnp.float32) + bias_in
    act_val, act_slope = gelu_pair(pre_act)
    hidden = act_val.astype(jnp.bfloat16)
    branch = jnp.dot(hidden, weight_out, preferred_element_type=jnp.float32) + bias_out
    upstream = grad_view.reshape(-1, channels).astype(jnp.float32)
    grad_branch = upstream * layer_scale
    grad_branch_b = grad_branch.astype(jnp.bfloat16)
    grad_hidden = lax.dot_general(
        grad_branch_b, weight_out, contract_last, preferred_element_type=jnp.float32
    )
    grad_pre = (grad_hidden * act_slope).astype(jnp.bfloat16)
    grad_scaled = lax.dot_general(
        grad_pre, weight_in, contract_last, preferred_element_type=jnp.float32
    )
    grad_normed = grad_scaled.reshape(row_count, col_count, channels) * norm_gain
    grad_conv = (
        grad_normed
        - jnp.mean(grad_normed, axis=2, keepdims=True)
        - normed * jnp.mean(grad_normed * normed, axis=2, keepdims=True)
    ) * inv_std
    flat_parts = [
        flat_in,
        hidden,
        branch,
        upstream,
        grad_branch,
        grad_branch_b,
        grad_pre,
        grad_scaled,
    ]
    return (flat_parts, normed, grad_conv)


def per_device(
    feature_map,
    cotangent,
    kernel,
    kernel_bias,
    norm_gain,
    norm_bias,
    weight_in,
    bias_in,
    weight_out,
    bias_out,
    layer_scale,
):
    tile_rows, tile_cols, channels = feature_map.shape
    contract_first = (((0,), (0,)), ((), ()))
    padded = with_halo(feature_map, (("row", 0), ("col", 1)), 3)
    flat_parts, normed_full, grad_conv_full = forward_back(
        padded,
        cotangent,
        kernel,
        kernel_bias,
        norm_gain,
        norm_bias,
        weight_in,
        bias_in,
        weight_out,
        bias_out,
        layer_scale,
    )
    trimmed = [element for element in flat_parts]
    flat_in, hidden, branch, upstream, grad_branch, grad_branch_b, grad_pre, grad_scaled = trimmed
    grad_w_in = lax.dot_general(
        flat_in, grad_pre, contract_first, preferred_element_type=jnp.float32
    )
    grad_b_in = jnp.sum(grad_pre.astype(jnp.float32), axis=0)
    grad_w_out = lax.dot_general(
        hidden, grad_branch_b, contract_first, preferred_element_type=jnp.float32
    )
    grad_b_out = jnp.sum(grad_branch, axis=0)
    grad_scale = jnp.sum(upstream * branch, axis=0)
    grad_pad = with_halo(grad_conv_full, (("row", 0), ("col", 1)), 3)
    grad_gain = jnp.sum(grad_scaled * normed_full.reshape(-1, channels), axis=0)
    grad_shift = jnp.sum(grad_scaled, axis=0)
    tap_sums = []
    for tap_index in range(KS * KS):
        row_off, col_off = divmod(tap_index, KS)
        tap_sums.append(
            jnp.sum(
                padded[row_off : row_off + tile_rows, col_off : col_off + tile_cols]
                * grad_conv_full,
                axis=(0, 1),
            )
        )
    grad_kernel = jnp.stack(tap_sums)
    grad_kbias = jnp.sum(grad_conv_full, axis=(0, 1))
    running_input = cotangent.astype(jnp.float32)
    for tap_index in range(KS * KS):
        row_off, col_off = divmod(tap_index, KS)
        running_input = (
            running_input
            + grad_pad[6 - row_off : 6 - row_off + tile_rows, 6 - col_off : 6 - col_off + tile_cols]
            * kernel[tap_index]
        )
    totals = lax.psum(
        (
            grad_kernel,
            grad_kbias,
            grad_gain,
            grad_shift,
            grad_w_in,
            grad_b_in,
            grad_w_out,
            grad_b_out,
            grad_scale,
        ),
        ("row", "col"),
    )
    divisor = 4.0 * lax.axis_size("row")
    return (
        running_input.astype(jnp.bfloat16),
        totals[0] / divisor,
        totals[1] / divisor,
        totals[2] / divisor,
        totals[3] / divisor,
        totals[4] / divisor,
        totals[5] / divisor,
        totals[6] / divisor,
        totals[7] / divisor,
        totals[8] / divisor,
    )


def solution(mesh):
    in_specs = (
        P(("groups", "row"), "col", None),
        P(("groups", "row"), "col", None),
        P(),
        P(),
        P(),
        P(),
        P(),
        P(),
        P(),
        P(),
        P(),
    )
    out_specs = (
        P(("groups", "row"), "col", None),
        P("groups", None),
        P("groups"),
        P("groups"),
        P("groups"),
        P("groups", None),
        P("groups"),
        P("groups", None),
        P("groups"),
        P("groups"),
    )
    return jax.shard_map(
        per_device, mesh=mesh, in_specs=in_specs, out_specs=out_specs, check_vma=False
    )
```

profile of v0, /device:TPU:0, one launch (start us, length us, event | category | flops | bytes accessed | tf_op | source)
XLA Modules:
  0.0 222.0 jit_solution(7255380133505937466)
XLA Ops:
  7.3 0.9 fusion.213
  8.2 4.9 %collective-permute-start = (bf16[3,32,256]{2,1,0:T(8,128)(2,1)S(1)}, bf16[3,32,256]{2,1,0:T(8,128)(2,1)S(1)}, u32[]{:S(2)}, u32[]{:S(2)}) collective-permute-start(bf16[3,32,256]{2,1,0:T(8,128)(2,1)S(1)} %get-tuple-element.95), channel_id=1, source_target_pairs={{0,2},{2,4},{4,6},{6,8},{8,10},{10,12},{12,14},{1,3},{3,5},{5,7},{... | collective-permute-start | bytes 147464 | tf_op jit(solution)/shard_map/ppermute | solution.py:14
  13.1 1.3 collective-permute-start.1
  14.4 1.0 fusion.214
  15.4 1.0 fusion.215
  16.6 1.0 fusion.165
  17.6 0.9 fusion.216
  18.7 1.0 constant_dynamic-update-slice_fusion.3
  19.8 1.5 collective-permute-start.2
  21.3 1.3 collective-permute-start.3
  22.6 0.7 multiply_reduce_fusion
  23.3 1.1 collective-permute-done.3
  24.4 5.6 %fusion.209 = (f32[16,32]{1,0:T(8,128)S(1)}, f32[16,32,256]{2,1,0:T(8,128)S(1)}) fusion(f32[256]{0:T(256)S(1)} %copy-done.84, f32[256]{0:T(256)S(1)} %bitcast.221, bf16[22,3,256]{2,1,0:T(4,128)(2,1)S(1)} %collective-permute-done.3, bf16[22,32,256]{2,1,0:T(8,128)(2,1)S(1)} %get-tuple-element.148, f32[256]{0:T(256)S(1)} %bitcast.223, f32[256]{0:T(256)S(1)} %bitcast.129, ...), kind=kLoop, calls=%fused_computation.480 | loop fusion | flops 35913216 | bytes 2840576 | tf_op jit(solution)/shard_map/reduce_sum | solution.py:56
  30.8 1.6 multiply_convert_fusion
  32.4 1.9 convert_reduce_fusion
  34.3 1.4 fusion.217
  35.8 1.1 fusion.208
  37.1 1.7 fusion.158
  38.8 0.9 fusion.155
  39.8 1.5 fusion.218
  41.3 1.5 fusion.7
  45.5 63.6 %all-reduce = (f32[49,256]{1,0:T(8,128)S(1)}, f32[256]{0:T(256)S(1)}, f32[256]{0:T(256)S(1)}, f32[256]{0:T(256)S(1)}, f32[1024]{0:T(1024)S(1)}, /*index=5*/f32[256]{0:T(256)S(1)}, f32[256]{0:T(256)S(1)}) all-reduce(f32[49,256]{1,0:T(8,128)S(1)} %stack.199, ...), channel_id=1, replica_groups=mesh['groups'=2,'row'=8,'col'=2] {'row','col'}, use_global_device_ids=true, to_apply=%region_53.0 | all-reduce | flops 14848 | bytes 118784 | tf_op jit(solution)/shard_map/psum | solution.py:156
  109.0 0.6 broadcast_multiply_fusion.2
  110.3 1.3 collective-permute-start.4
  111.6 1.3 collective-permute-start.5
  114.8 3.3 %collective-permute-done.5 = f32[3,32,256]{2,1,0:T(8,128)S(1)} collective-permute-done((f32[3,32,256]{2,1,0:T(8,128)S(1)}, f32[3,32,256]{2,1,0:T(8,128)S(1)}, u32[]{:S(2)}, u32[]{:S(2)}) %collective-permute-start.5) | collective-permute-done | bytes 98336 | tf_op jit(solution)/shard_map/ppermute | solution.py:17
  118.1 1.3 collective-permute-start.6
  119.4 3.2 %collective-permute-start.7 = (f32[22,3,256]{2,1,0:T(4,128)S(1)}, f32[22,3,256]{2,1,0:T(4,128)S(1)}, u32[]{:S(2)}, u32[]{:S(2)}) collective-permute-start(f32[22,3,256]{2,1,0:T(4,128)S(1)} %get-tuple-element.86), channel_id=1, source_target_pairs={{0,1},{2,3},{4,5},{6,7},{8,9},{10,11},{12,13},{14,15},{16,17},{18,... | collective-permute-start | bytes 202760 | tf_op jit(solution)/shard_map/ppermute | solution.py:14
  123.8 4.7 %fusion.167 = bf16[16,32,256]{2,1,0:T(8,128)(2,1)} fusion(f32[22,35,256]{2,1,0:T(8,128)S(1)} %get-tuple-element.84, f32[16,32,256]{2,1,0:T(8,128)S(1)} %get-tuple-element.78, f32[3,32,256]{2,1,0:T(8,128)S(1)} %collective-permute-done.4, f32[22,35,256]{2,1,0:T(8,128)S(1)} %get-tuple-element.83, f32[3,32,256]{2,1,0:T(8,128)S(1)} %collective-permute-done.5, ...), kind=kLoop, calls=%fused_computation.374 | loop fusion | flops 13893632 | bytes 23315456 | tf_op jit(solution)/shard_map/convert_element_type | solution.py:172
  128.5 83.2 %all-reduce.4.cloned.1.call-done = (f32[256,1024]{1,0:T(8,128)}, f32[1024,256]{1,0:T(8,128)}) async-done(((f32[256,1024]{1,0:T(8,128)}, f32[1024,256]{1,0:T(8,128)}), (f32[256,1024]{1,0:T(8,128)}, f32[1024,256]{1,0:T(8,128)})) %all-reduce.4.cloned.1.call-update) | async-done | bytes 2097168 | tf_op jit(solution)/shard_map/psum | solution.py:156
  211.7 2.4 %broadcast_multiply_fusion = f32[1024,256]{1,0:T(8,128)} fusion(f32[1024,256]{1,0:T(8,128)} %get-tuple-element.77), kind=kLoop, calls=%fused_computation.366 | loop fusion | flops 262144 | bytes 2097152 | tf_op jit(solution)/shard_map/div | solution.py:179
  214.0 1.1 broadcast_multiply_fusion.1
  (207 shorter events, 6.6 us)
Async XLA Ops:
  7.2 23.6 %copy-start = (bf16[256,1024]{1,0:T(8,128)(2,1)S(1)}, bf16[256,1024]{1,0:T(8,128)(2,1)}, u32[]{:S(2)}) copy-start(bf16[256,1024]{1,0:T(8,128)(2,1)} %param.17) | copy-start | bytes 1572868
  7.2 17.2 %copy-start.3 = (bf16[16,32,256]{2,1,0:T(8,128)(2,1)S(1)}, bf16[16,32,256]{2,1,0:T(8,128)(2,1)}, u32[]{:S(2)}) copy-start(bf16[16,32,256]{2,1,0:T(8,128)(2,1)} %param.11) | copy-start | bytes 786436
  7.2 15.4 %copy-start.4 = (bf16[16,32,256]{2,1,0:T(8,128)(2,1)S(1)}, bf16[16,32,256]{2,1,0:T(8,128)(2,1)}, u32[]{:S(2)}) copy-start(bf16[16,32,256]{2,1,0:T(8,128)(2,1)} %param.12) | copy-start | bytes 786436
  7.2 15.3 %copy-start.63 = (f32[256]{0:T(256)S(1)}, f32[256]{0:T(256)}, u32[]{:S(2)}) copy-start(f32[256]{0:T(256)} %param.21) | copy-start | bytes 3076
  7.2 17.1 %copy-start.84 = (f32[256]{0:T(256)S(1)}, f32[256]{0:T(256)}, u32[]{:S(2)}) copy-start(f32[256]{0:T(256)} %param.14) | copy-start | bytes 3076
  7.2 204.4 %all-reduce.4.cloned.1.call-start = ((), (), s32[]{:S(2)}) async-start(), calls=%async_computation | async-start | bytes 4194304 | tf_op jit(solution)/shard_map/psum | solution.py:156
  8.2 10.5 %collective-permute-start = (bf16[3,32,256]{2,1,0:T(8,128)(2,1)S(1)}, bf16[3,32,256]{2,1,0:T(8,128)(2,1)S(1)}, u32[]{:S(2)}, u32[]{:S(2)}) collective-permute-start(bf16[3,32,256]{2,1,0:T(8,128)(2,1)S(1)} %get-tuple-element.95), channel_id=1, source_target_pairs={{0,2},{2,4},{4,6},{6,8},{8,10},{10,12},{12,14},{1,3},{3,5},{5,7},{... | collective-permute-start | bytes 147464 | tf_op jit(solution)/shard_map/ppermute | solution.py:14
  13.1 6.6 %collective-permute-start.1 = (bf16[3,32,256]{2,1,0:T(8,128)(2,1)S(1)}, bf16[3,32,256]{2,1,0:T(8,128)(2,1)S(1)}, u32[]{:S(2)}, u32[]{:S(2)}) collective-permute-start(bf16[3,32,256]{2,1,0:T(8,128)(2,1)S(1)} %get-tuple-element.94), channel_id=1, source_target_pairs={{2,0},{4,2},{6,4},{8,6},{10,8},{12,10},{14,12},{3,1},{5,3},{7,5},{... | collective-permute-start | bytes 147464 | tf_op jit(solution)/shard_map/ppermute | solution.py:17
  16.4 13.6 %copy-start.10 = (f32[1,256]{1,0:T(1,128)}, f32[1,256]{1,0:T(1,128)S(1)}, u32[]{:S(2)}) copy-start(f32[1,256]{1,0:T(1,128)S(1)} %get-tuple-element.119) | copy-start | bytes 3076
  16.4 13.6 %copy-start.12 = (f32[1,256]{1,0:T(1,128)}, f32[1,256]{1,0:T(1,128)S(1)}, u32[]{:S(2)}) copy-start(f32[1,256]{1,0:T(1,128)S(1)} %get-tuple-element.120) | copy-start | bytes 3076
  16.4 13.6 %copy-start.14 = (f32[1,256]{1,0:T(1,128)}, f32[1,256]{1,0:T(1,128)S(1)}, u32[]{:S(2)}) copy-start(f32[1,256]{1,0:T(1,128)S(1)} %get-tuple-element.121) | copy-start | bytes 3076
  16.5 13.6 %copy-start.16 = (f32[1,256]{1,0:T(1,128)}, f32[1,256]{1,0:T(1,128)S(1)}, u32[]{:S(2)}) copy-start(f32[1,256]{1,0:T(1,128)S(1)} %get-tuple-element.122) | copy-start | bytes 3076
  16.5 13.6 %copy-start.18 = (f32[1,256]{1,0:T(1,128)}, f32[1,256]{1,0:T(1,128)S(1)}, u32[]{:S(2)}) copy-start(f32[1,256]{1,0:T(1,128)S(1)} %get-tuple-element.123) | copy-start | bytes 3076
  16.5 13.6 %copy-start.20 = (f32[1,256]{1,0:T(1,128)}, f32[1,256]{1,0:T(1,128)S(1)}, u32[]{:S(2)}) copy-start(f32[1,256]{1,0:T(1,128)S(1)} %get-tuple-element.124) | copy-start | bytes 3076
  16.5 13.6 %copy-start.22 = (f32[1,256]{1,0:T(1,128)}, f32[1,256]{1,0:T(1,128)S(1)}, u32[]{:S(2)}) copy-start(f32[1,256]{1,0:T(1,128)S(1)} %get-tuple-element.125) | copy-start | bytes 3076
  16.5 13.6 %copy-start.24 = (f32[1,256]{1,0:T(1,128)}, f32[1,256]{1,0:T(1,128)S(1)}, u32[]{:S(2)}) copy-start(f32[1,256]{1,0:T(1,128)S(1)} %get-tuple-element.126) | copy-start | bytes 3076
  16.5 13.6 %copy-start.26 = (f32[1,256]{1,0:T(1,128)}, f32[1,256]{1,0:T(1,128)S(1)}, u32[]{:S(2)}) copy-start(f32[1,256]{1,0:T(1,128)S(1)} %get-tuple-element.127) | copy-start | bytes 3076
  16.5 13.6 %copy-start.28 = (f32[1,256]{1,0:T(1,128)}, f32[1,256]{1,0:T(1,128)S(1)}, u32[]{:S(2)}) copy-start(f32[1,256]{1,0:T(1,128)S(1)} %get-tuple-element.128) | copy-start | bytes 3076
  16.5 13.6 %copy-start.30 = (f32[1,256]{1,0:T(1,128)}, f32[1,256]{1,0:T(1,128)S(1)}, u32[]{:S(2)}) copy-start(f32[1,256]{1,0:T(1,128)S(1)} %get-tuple-element.129) | copy-start | bytes 3076
  16.5 13.6 %copy-start.32 = (f32[1,256]{1,0:T(1,128)}, f32[1,256]{1,0:T(1,128)S(1)}, u32[]{:S(2)}) copy-start(f32[1,256]{1,0:T(1,128)S(1)} %get-tuple-element.130) | copy-start | bytes 3076
  16.5 13.6 %copy-start.34 = (f32[1,256]{1,0:T(1,128)}, f32[1,256]{1,0:T(1,128)S(1)}, u32[]{:S(2)}) copy-start(f32[1,256]{1,0:T(1,128)S(1)} %get-tuple-element.131) | copy-start | bytes 3076
  16.6 13.6 %copy-start.36 = (f32[1,256]{1,0:T(1,128)}, f32[1,256]{1,0:T(1,128)S(1)}, u32[]{:S(2)}) copy-start(f32[1,256]{1,0:T(1,128)S(1)} %get-tuple-element.132) | copy-start | bytes 3076
  16.6 13.6 %copy-start.38 = (f32[1,256]{1,0:T(1,128)}, f32[1,256]{1,0:T(1,128)S(1)}, u32[]{:S(2)}) copy-start(f32[1,256]{1,0:T(1,128)S(1)} %get-tuple-element.133) | copy-start | bytes 3076
  17.6 14.8 %copy-start.6 = (bf16[512,256]{1,0:T(8,128)(2,1)}, bf16[512,256]{1,0:T(8,128)(2,1)S(1)}, u32[]{:S(2)}) copy-start(bf16[512,256]{1,0:T(8,128)(2,1)S(1)} %fusion.165) | copy-start | bytes 786436
  18.5 11.6 %copy-start.40 = (f32[1,256]{1,0:T(1,128)}, f32[1,256]{1,0:T(1,128)S(1)}, u32[]{:S(2)}) copy-start(f32[1,256]{1,0:T(1,128)S(1)} %get-tuple-element.134) | copy-start | bytes 3076
  18.5 11.6 %copy-start.42 = (f32[1,256]{1,0:T(1,128)}, f32[1,256]{1,0:T(1,128)S(1)}, u32[]{:S(2)}) copy-start(f32[1,256]{1,0:T(1,128)S(1)} %get-tuple-element.135) | copy-start | bytes 3076
  19.8 3.5 %collective-permute-start.2 = (bf16[22,3,256]{2,1,0:T(4,128)(2,1)S(1)}, bf16[22,3,256]{2,1,0:T(4,128)(2,1)S(1)}, u32[]{:S(2)}, u32[]{:S(2)}) collective-permute-start(bf16[22,3,256]{2,1,0:T(4,128)(2,1)S(1)} %get-tuple-element.89), channel_id=1, source_target_pairs={{0,1},{2,3},{4,5},{6,7},{8,9},{10,11},{12,13},{14,15},{16,17},{18,... | collective-permute-start | bytes 101384 | tf_op jit(solution)/shard_map/ppermute | solution.py:14
  21.3 3.1 %collective-permute-start.3 = (bf16[22,3,256]{2,1,0:T(4,128)(2,1)S(1)}, bf16[22,3,256]{2,1,0:T(4,128)(2,1)S(1)}, u32[]{:S(2)}, u32[]{:S(2)}) collective-permute-start(bf16[22,3,256]{2,1,0:T(4,128)(2,1)S(1)} %get-tuple-element.90), channel_id=1, source_target_pairs={{1,0},{3,2},{5,4},{7,6},{9,8},{11,10},{13,12},{15,14},{17,16},{19,... | collective-permute-start | bytes 101384 | tf_op jit(solution)/shard_map/ppermute | solution.py:17
  110.3 4.5 %collective-permute-start.4 = (f32[3,32,256]{2,1,0:T(8,128)S(1)}, f32[3,32,256]{2,1,0:T(8,128)S(1)}, u32[]{:S(2)}, u32[]{:S(2)}) collective-permute-start(f32[3,32,256]{2,1,0:T(8,128)S(1)} %get-tuple-element.87), channel_id=1, source_target_pairs={{0,2},{2,4},{4,6},{6,8},{8,10},{10,12},{12,14},{1,3},{3,5},{5,7},{... | collective-permute-start | bytes 294920 | tf_op jit(solution)/shard_map/ppermute | solution.py:14
  111.6 6.5 %collective-permute-start.5 = (f32[3,32,256]{2,1,0:T(8,128)S(1)}, f32[3,32,256]{2,1,0:T(8,128)S(1)}, u32[]{:S(2)}, u32[]{:S(2)}) collective-permute-start(f32[3,32,256]{2,1,0:T(8,128)S(1)} %get-tuple-element.88), channel_id=1, source_target_pairs={{2,0},{4,2},{6,4},{8,6},{10,8},{12,10},{14,12},{3,1},{5,3},{7,5},{... | collective-permute-start | bytes 294920 | tf_op jit(solution)/shard_map/ppermute | solution.py:17
  118.1 5.1 %collective-permute-start.6 = (f32[22,3,256]{2,1,0:T(4,128)S(1)}, f32[22,3,256]{2,1,0:T(4,128)S(1)}, u32[]{:S(2)}, u32[]{:S(2)}) collective-permute-start(f32[22,3,256]{2,1,0:T(4,128)S(1)} %get-tuple-element.85), channel_id=1, source_target_pairs={{1,0},{3,2},{5,4},{7,6},{9,8},{11,10},{13,12},{15,14},{17,16},{19,... | collective-permute-start | bytes 202760 | tf_op jit(solution)/shard_map/ppermute | solution.py:17
  119.4 4.0 %collective-permute-start.7 = (f32[22,3,256]{2,1,0:T(4,128)S(1)}, f32[22,3,256]{2,1,0:T(4,128)S(1)}, u32[]{:S(2)}, u32[]{:S(2)}) collective-permute-start(f32[22,3,256]{2,1,0:T(4,128)S(1)} %get-tuple-element.86), channel_id=1, source_target_pairs={{0,1},{2,3},{4,5},{6,7},{8,9},{10,11},{12,13},{14,15},{16,17},{18,... | collective-permute-start | bytes 202760 | tf_op jit(solution)/shard_map/ppermute | solution.py:14
  (65 other events, 457.3 us)
Sparse Core Ops, SparseCore 0:
  113.6 98.0 all-reduce.3
where the time goes:
time: 223 us; the launch traced here: 222 us
  waiting for transfers between devices  88.3 us (40%)
  blocking collectives  63.6 us (29%)
  other arithmetic  24 us (11%)
  starting transfers between devices  16 us (7%)
  between operations  15.5 us (7%)
  matrix products  8.97 us (4%)
  local copies, waits for them, and re-layouts  5.63 us (3%)
    psum x1, waiting for transfers between devices, per_device(): lax.psum((grad_kernel, grad_kbias, grad_gain, grad_shift, grad_w_in, grad...  83.2 us
    psum x1, blocking collectives, per_device(): lax.psum((grad_kernel, grad_kbias, grad_gain, grad_shift, grad_w_in, grad...  63.6 us
    ppermute x4, starting transfers between devices, with_halo(): lax.ppermute(lax.slice_in_dim(block, block.shape[dim] - width, None, axis...  10.8 us
    reduce_sum x1, other arithmetic, forward_back(): centred = conv_out - jnp.mean(conv_out, axis=2, keepdims=True)  5.65 us
    ppermute x4, starting transfers between devices, with_halo(): lax.ppermute(lax.slice_in_dim(block, 0, width, axis=dim), axis, backward)  5.17 us
    reduce_sum x6, other arithmetic, per_device(): jnp.sum(padded[row_off:row_off + tile_rows, col_off:col_off + tile_cols]...  4.8 us
    convert_element_type x1, other arithmetic, per_device(): running_input.astype(jnp.bfloat16)  4.72 us
  transfers between devices with their start and end apart: 9, of which 5 were waited for; matrix products, arithmetic and copies ran while one was open for 6% of the time, Pallas kernels for 0%

commit v1 on v0

--- a/solution.py
+++ b/solution.py
@@ -1,6 +1,9 @@
+import functools
+
 import jax
 import jax.numpy as jnp
 from jax import lax
+import numpy as np
 from jax.sharding import PartitionSpec as P
 
 KS = 7
@@ -90,7 +93,95 @@
     return (flat_parts, normed, grad_conv)
 
 
+def ring_order(coords):
+    count = len(coords)
+    varying = [k for k in range(len(coords[0])) if len({c[k] for c in coords}) > 1]
+    if len(varying) != 2:
+        return sorted(range(count), key=lambda r: coords[r])
+    ranks = []
+    for k in varying:
+        values = sorted({c[k] for c in coords})
+        ranks.append({v: i for i, v in enumerate(values)})
+    grid = {(ranks[0][c[varying[0]]], ranks[1][c[varying[1]]]): r for r, c in enumerate(coords)}
+    size_a, size_b = len(ranks[0]), len(ranks[1])
+    swap = size_a % 2 == 1
+    if swap:
+        size_a, size_b = size_b, size_a
+    if size_a % 2 == 1 or size_a * size_b != count:
+        return list(range(count))
+    cycle = []
+    for i in range(size_a):
+        cols = range(1, size_b) if i % 2 == 0 else range(size_b - 1, 0, -1)
+        cycle += [(i, j) for j in cols]
+    cycle += [(i, 0) for i in range(size_a - 1, -1, -1)]
+    if swap:
+        cycle = [(j, i) for i, j in cycle]
+    return [grid[cell] for cell in cycle]
+
+
+def ring_position(axis, order):
+    position_of = [0] * len(order)
+    for position, member in enumerate(order):
+        position_of[member] = position
+    return jnp.asarray(position_of, jnp.int32)[lax.axis_index(axis)]
+
+
+def ring_pairs(order, step):
+    count = len(order)
+    return [(order[i], order[(i + step) % count]) for i in range(count)]
+
+
+def ring_reduce_scatter(block, axis, order, ways):
+    count = len(order)
+    if count == 1:
+        return [block]
+    here = ring_position(axis, order)
+    part = block.shape[0] // (ways * count)
+    chunks = block.reshape(ways, count, part, block.shape[1])
+    signs = (1, -1)[:ways]
+
+    def take(way, index):
+        return lax.dynamic_index_in_dim(chunks[way], index % count, axis=0, keepdims=False)
+
+    held = [take(way, here) for way in range(ways)]
+    for step in range(count - 1):
+        held = [
+            lax.ppermute(held[way], axis, ring_pairs(order, signs[way]))
+            + take(way, here - signs[way] * (1 + step))
+            for way in range(ways)
+        ]
+    return held
+
+
+def ring_all_gather(held, axis, order):
+    count = len(order)
+    if count == 1:
+        return held[0]
+    here = ring_position(axis, order)
+    signs = (1, -1)[: len(held)]
+    gathered = []
+    for way, piece in enumerate(held):
+        sign = signs[way]
+        full = jnp.zeros((count,) + piece.shape, piece.dtype)
+        full = lax.dynamic_update_index_in_dim(full, piece, (here + sign) % count, axis=0)
+        for step in range(count - 1):
+            piece = lax.ppermute(piece, axis, ring_pairs(order, sign))
+            full = lax.dynamic_update_index_in_dim(full, piece, (here - sign * step) % count, axis=0)
+        gathered.append(full)
+    stacked = jnp.stack(gathered)
+    return stacked.reshape(-1, stacked.shape[-1])
+
+
+def ring_all_reduce(block, row_order, col_order):
+    block = ring_reduce_scatter(block, "col", col_order, 1)[0]
+    held = ring_reduce_scatter(block, "row", row_order, 2)
+    block = ring_all_gather(held, "row", row_order)
+    return ring_all_gather([block], "col", col_order)
+
+
 def per_device(
+    row_order,
+    col_order,
     feature_map,
     cotangent,
     kernel,
@@ -122,7 +213,7 @@
     trimmed = [element for element in flat_parts]
     flat_in, hidden, branch, upstream, grad_branch, grad_branch_b, grad_pre, grad_scaled = trimmed
     grad_w_in = lax.dot_general(
-        flat_in, grad_pre, contract_first, preferred_element_type=jnp.float32
+        grad_pre, flat_in, contract_first, preferred_element_type=jnp.float32
     )
     grad_b_in = jnp.sum(grad_pre.astype(jnp.float32), axis=0)
     grad_w_out = lax.dot_general(
@@ -143,7 +234,7 @@
                 axis=(0, 1),
             )
         )
-    grad_kernel = jnp.stack(tap_sums)
+    grad_kernel = lax.optimization_barrier(jnp.stack(tap_sums))
     grad_kbias = jnp.sum(grad_conv_full, axis=(0, 1))
     running_input = cotangent.astype(jnp.float32)
     for tap_index in range(KS * KS):
@@ -153,32 +244,44 @@
             + grad_pad[6 - row_off : 6 - row_off + tile_rows, 6 - col_off : 6 - col_off + tile_cols]
             * kernel[tap_index]
         )
-    totals = lax.psum(
-        (
-            grad_kernel,
-            grad_kbias,
-            grad_gain,
-            grad_shift,
-            grad_w_in,
-            grad_b_in,
-            grad_w_out,
-            grad_b_out,
-            grad_scale,
-        ),
-        ("row", "col"),
-    )
     divisor = 4.0 * lax.axis_size("row")
+    pieces = [
+        grad_w_in,
+        grad_w_out,
+        grad_kernel,
+        grad_kbias,
+        grad_gain,
+        grad_shift,
+        grad_b_in,
+        grad_b_out,
+        grad_scale,
+    ]
+    flat = [piece.reshape(-1, channels) for piece in pieces]
+    rows = sum(piece.shape[0] for piece in flat)
+    unit = 2 * 8 * len(row_order) * len(col_order)
+    flat.append(jnp.zeros(((-rows) % unit, channels), jnp.float32))
+    packed = ring_all_reduce(jnp.concatenate(flat, axis=0), row_order, col_order)
+    totals = []
+    at = 0
+    for piece in pieces:
+        count = piece.size // channels
+        part = packed[at : at + count]
+        if piece is grad_w_in:
+            part = part.T
+        totals.append(part.reshape(piece.shape if piece is not grad_w_in else (channels, -1)) / divisor)
+        at += count
+    (w_in, w_out, g_kernel, g_kbias, g_gain, g_shift, g_b_in, g_b_out, g_scale) = totals
     return (
         running_input.astype(jnp.bfloat16),
-        totals[0] / divisor,
-        totals[1] / divisor,
-        totals[2] / divisor,
-        totals[3] / divisor,
-        totals[4] / divisor,
-        totals[5] / divisor,
-        totals[6] / divisor,
-        totals[7] / divisor,
-        totals[8] / divisor,
+        g_kernel,
+        g_kbias,
+        g_gain,
+        g_shift,
+        w_in,
+        g_b_in,
+        w_out,
+        g_b_out,
+        g_scale,
     )
 
 
@@ -208,6 +311,12 @@
         P("groups"),
         P("groups"),
     )
+    devices = mesh.devices
+    row_at = mesh.axis_names.index("row")
+    col_at = mesh.axis_names.index("col")
+    row_members = np.moveaxis(devices, row_at, 0).reshape(devices.shape[row_at], -1)[:, 0]
+    row_order = ring_order([tuple(device.coords) for device in row_members])
+    col_order = list(range(devices.shape[col_at]))
     return jax.shard_map(
-        per_device, mesh=mesh, in_specs=in_specs, out_specs=out_specs, check_vma=False
-    )
+        functools.partial(per_device, row_order, col_order), mesh=mesh, in_specs=in_specs, out_specs=out_specs, check_vma=False
+    )

time: 223 us -> 153 us (0.69)
  blocking collectives: 63.6 us -> 0 us
  waiting for transfers between devices: 88.3 us -> 31.3 us
  starting transfers between devices: 16 us -> 56.7 us
  local copies, waits for them, and re-layouts: 5.63 us -> 17.2 us
    psum x1 -> x0, waiting for transfers between devices: 83.2 us -> none  [per_device(): lax.psum((grad_kernel, grad_kbias, grad_gain, grad_shift, grad_w_in, grad...]
    psum x1 -> x0, blocking collectives: 63.6 us -> none  [per_device(): lax.psum((grad_kernel, grad_kbias, grad_gain, grad_shift, grad_w_in, grad...]
    ppermute x0 -> x30, starting transfers between devices: none -> 37.9 us  [the longest x15 19.9 us: ring_reduce_scatter(): lax.ppermute(held[way], axis, ring_pairs(order, signs[way]))]
    ppermute x0 -> x30, waiting for transfers between devices: none -> 30.1 us  [the longest x15 15.5 us: ring_all_gather(): piece = lax.ppermute(piece, axis, ring_pairs(order, sign))]
    concatenate x0 -> x1, local copies, waits for them, and re-layouts: none -> 5.25 us  [per_device(): jnp.concatenate(flat, axis=0)]
    div x7 -> x3, other arithmetic: 6.37 us -> 2.32 us  [per_device(): part.reshape(piece.shape if piece is not grad_w_in else (channels, -1))]
    ppermute x4, waiting for transfers between devices: 4.42 us -> 1.12 us  [with_halo(): lax.ppermute(lax.slice_in_dim(block, 0, width, axis=dim), axis, backward)]
    ppermute x4, starting transfers between devices: 10.8 us -> 13.7 us  [with_halo(): lax.ppermute(lax.slice_in_dim(block, block.shape[dim] - width, None, axis...]
  transfers between devices with their start and end apart: 9 -> 38, of which waited for: 5 -> 28; matrix products, arithmetic and copies ran while one was open for 6% -> 11% of each run, Pallas kernels for 0% -> 0%
where the time goes in v1:
time: 153 us; the launch traced here: 152 us
  starting transfers between devices  56.7 us (37%)
  waiting for transfers between devices  31.3 us (20%)
  other arithmetic  23.5 us (15%)
  local copies, waits for them, and re-layouts  17.2 us (11%)
  between operations  13.8 us (9%)
  matrix products  8.95 us (6%)
    ppermute x15, starting transfers between devices, ring_reduce_scatter(): lax.ppermute(held[way], axis, ring_pairs(order, signs[way]))  19.9 us
    ppermute x15, starting transfers between devices, ring_all_gather(): piece = lax.ppermute(piece, axis, ring_pairs(order, sign))  18 us
    ppermute x15, waiting for transfers between devices, ring_all_gather(): piece = lax.ppermute(piece, axis, ring_pairs(order, sign))  15.5 us
    ppermute x15, waiting for transfers between devices, ring_reduce_scatter(): lax.ppermute(held[way], axis, ring_pairs(order, signs[way]))  14.6 us
    ppermute x4, starting transfers between devices, with_halo(): lax.ppermute(lax.slice_in_dim(block, block.shape[dim] - width, None, axis...  13.7 us
    reduce_sum x1, other arithmetic, forward_back(): centred = conv_out - jnp.mean(conv_out, axis=2, keepdims=True)  5.62 us
    convert_element_type x1, other arithmetic, per_device(): running_input.astype(jnp.bfloat16)  5.57 us
    concatenate x1, local copies, waits for them, and re-layouts, per_device(): jnp.concatenate(flat, axis=0)  5.25 us
  transfers between devices with their start and end apart: 38, of which 28 were waited for; matrix products, arithmetic and copies ran while one was open for 11% of the time, Pallas kernels for 0%

profile of v1, /device:TPU:0, one launch (start us, length us, event | category | flops | bytes accessed | tf_op | source)
XLA Modules:
  0.0 151.5 jit_solution(8816093850049559426)
XLA Ops:
  1.6 4.9 %collective-permute-start = (bf16[3,32,256]{2,1,0:T(8,128)(2,1)S(1)}, bf16[3,32,256]{2,1,0:T(8,128)(2,1)S(1)}, u32[]{:S(2)}, u32[]{:S(2)}) collective-permute-start(bf16[3,32,256]{2,1,0:T(8,128)(2,1)S(1)} %get-tuple-element.109), channel_id=1, source_target_pairs={{0,2},{2,4},{4,6},{6,8},{8,10},{10,12},{12,14},{1,3},{3,5},{5,7},{... | collective-permute-start | bytes 147464 | tf_op jit(solution)/shard_map/ppermute | solution.py:17
  18.0 5.6 %fusion.211 = (f32[16,32]{1,0:T(8,128)S(1)}, f32[16,32,256]{2,1,0:T(8,128)S(1)}) fusion(f32[256]{0:T(256)S(1)} %copy-done.90, f32[256]{0:T(256)S(1)} %bitcast.339, bf16[22,3,256]{2,1,0:T(4,128)(2,1)S(1)} %collective-permute-done.3, bf16[22,32,256]{2,1,0:T(8,128)(2,1)S(1)} %get-tuple-element.162, f32[256]{0:T(256)S(1)} %bitcast.341, f32[256]{0:T(256)S(1)} %bitcast.247, ...), kind=kLoop, calls=%fused_computation.519 | loop fusion | flops 35913216 | bytes 2840576 | tf_op jit(solution)/shard_map/reduce_sum | solution.py:59
  24.5 1.6 %multiply_convert_fusion = (bf16[512,1024]{1,0:T(8,128)(2,1)}, f32[512,1024]{1,0:T(8,128)S(1)}) fusion(f32[1024]{0:T(1024)S(1)} %copy-done.83, bf16[512,256]{1,0:T(8,128)(2,1)S(1)} %bitcast.243, bf16[256,1024]{1,0:T(8,128)(2,1)S(1)} %copy-done), kind=kOutput, calls=%fused_computation.48 | convolution fusion | flops 271581184 | bytes 3936256 | tf_op jit(solution)/shard_map/dot_general | solution.py:63
  26.1 1.9 %convert_reduce_fusion = (f32[1024]{0:T(1024)}, bf16[512,1024]{1,0:T(8,128)(2,1)S(1)}) fusion(f32[512,1024]{1,0:T(8,128)S(1)} %get-tuple-element.165, f32[1024]{0:T(1024)S(1)} %copy-done.83, bf16[512,256]{1,0:T(8,128)(2,1)S(1)} %fusion.166, bf16[1024,256]{1,0:T(8,128)(2,1)S(1)} %copy-done.92), kind=kOutput, calls=%fused_computation.47 | convolution fusion | flops 275250176 | bytes 3940352 | tf_op jit(solution)/shard_map/dot_general | solution.py:70
  36.6 1.5 fusion.7
  38.9 5.2 %concatenate.133 = f32[2304,256]{1,0:T(8,128)S(1)} concatenate(f32[1024,256]{1,0:T(8,128)} %fusion.220, f32[1024,256]{1,0:T(8,128)} %fusion.221, f32[49,256]{1,0:T(8,128)S(1)} %stack.239, f32[1,256]{1,0:T(1,128)S(1)} %bitcast.396, f32[1,256]{1,0:T(1,128)S(1)} %bitcast.395, f32[1,256]{1,0:T(1,128)S(1)} %bitcast.394, f32[4,256]{1,0:T(4,128)S(1)} %reshape.216, ...), dimensions={0} | concatenate | bytes 4718592 | tf_op jit(solution)/shard_map/concatenate | solution.py:263
  46.0 4.4 %collective-permute-start.4 = (f32[3,32,256]{2,1,0:T(8,128)}, f32[3,32,256]{2,1,0:T(8,128)S(1)}, u32[]{:S(2)}, u32[]{:S(2)}) collective-permute-start(f32[3,32,256]{2,1,0:T(8,128)} %get-tuple-element.101), channel_id=1, source_target_pairs={{0,2},{2,4},{4,6},{6,8},{8,10},{10,12},{12,14},{1,3},{3,5},{5,7},{... | collective-permute-start | bytes 294920 | tf_op jit(solution)/shard_map/ppermute | solution.py:17
  66.3 3.0 %collective-permute-start.7 = (f32[22,3,256]{2,1,0:T(4,128)S(1)}, f32[22,3,256]{2,1,0:T(4,128)S(1)}, u32[]{:S(2)}, u32[]{:S(2)}) collective-permute-start(f32[22,3,256]{2,1,0:T(4,128)S(1)} %get-tuple-element.100), channel_id=1, source_target_pairs={{0,1},{2,3},{4,5},{6,7},{8,9},{10,11},{12,13},{14,15},{16,17},{18,... | collective-permute-start | bytes 202760 | tf_op jit(solution)/shard_map/ppermute | solution.py:17
  70.9 4.6 %collective-permute-start.9 = (f32[72,256]{1,0:T(8,128)S(1)}, f32[72,256]{1,0:T(8,128)S(1)}, u32[]{:S(2)}, u32[]{:S(2)}) collective-permute-start(f32[72,256]{1,0:T(8,128)S(1)} %dynamic-slice_bitcast_fusion.2), channel_id=1, source_target_pairs={{4,8},{8,12},{12,14},{14,10},{10,6},{6,2},{2,0},{0,4},{5,9},{9,13}... | collective-permute-start | bytes 221192 | tf_op jit(solution)/shard_map/ppermute | solution.py:149
  75.6 2.0 %collective-permute-done.9 = f32[72,256]{1,0:T(8,128)S(1)} collective-permute-done((f32[72,256]{1,0:T(8,128)S(1)}, f32[72,256]{1,0:T(8,128)S(1)}, u32[]{:S(2)}, u32[]{:S(2)}) %collective-permute-start.9) | collective-permute-done | bytes 73760 | tf_op jit(solution)/shard_map/ppermute | solution.py:149
  77.5 2.4 %collective-permute-start.10 = (f32[72,256]{1,0:T(8,128)S(1)}, f32[72,256]{1,0:T(8,128)S(1)}, u32[]{:S(2)}, u32[]{:S(2)}) collective-permute-start(f32[72,256]{1,0:T(8,128)S(1)} %bitcast_add_fusion.14), channel_id=1, source_target_pairs={{4,8},{8,12},{12,14},{14,10},{10,6},{6,2},{2,0},{0,4},{5,9},{9,13}... | collective-permute-start | bytes 221192 | tf_op jit(solution)/shard_map/ppermute | solution.py:149
  80.0 1.9 %collective-permute-done.10 = f32[72,256]{1,0:T(8,128)S(1)} collective-permute-done((f32[72,256]{1,0:T(8,128)S(1)}, f32[72,256]{1,0:T(8,128)S(1)}, u32[]{:S(2)}, u32[]{:S(2)}) %collective-permute-start.10) | collective-permute-done | bytes 73760 | tf_op jit(solution)/shard_map/ppermute | solution.py:149
  82.0 2.5 %collective-permute-start.11 = (f32[72,256]{1,0:T(8,128)S(1)}, f32[72,256]{1,0:T(8,128)S(1)}, u32[]{:S(2)}, u32[]{:S(2)}) collective-permute-start(f32[72,256]{1,0:T(8,128)S(1)} %bitcast_add_fusion.13), channel_id=1, source_target_pairs={{4,8},{8,12},{12,14},{14,10},{10,6},{6,2},{2,0},{0,4},{5,9},{9,13}... | collective-permute-start | bytes 221192 | tf_op jit(solution)/shard_map/ppermute | solution.py:149
  84.6 2.5 %collective-permute-done.11 = f32[72,256]{1,0:T(8,128)S(1)} collective-permute-done((f32[72,256]{1,0:T(8,128)S(1)}, f32[72,256]{1,0:T(8,128)S(1)}, u32[]{:S(2)}, u32[]{:S(2)}) %collective-permute-start.11) | collective-permute-done | bytes 73760 | tf_op jit(solution)/shard_map/ppermute | solution.py:149
  87.1 2.1 %collective-permute-start.12 = (f32[72,256]{1,0:T(8,128)S(1)}, f32[72,256]{1,0:T(8,128)S(1)}, u32[]{:S(2)}, u32[]{:S(2)}) collective-permute-start(f32[72,256]{1,0:T(8,128)S(1)} %bitcast_add_fusion.12), channel_id=1, source_target_pairs={{4,8},{8,12},{12,14},{14,10},{10,6},{6,2},{2,0},{0,4},{5,9},{9,13}... | collective-permute-start | bytes 221192 | tf_op jit(solution)/shard_map/ppermute | solution.py:149
  89.9 1.6 %collective-permute-done.12 = f32[72,256]{1,0:T(8,128)S(1)} collective-permute-done((f32[72,256]{1,0:T(8,128)S(1)}, f32[72,256]{1,0:T(8,128)S(1)}, u32[]{:S(2)}, u32[]{:S(2)}) %collective-permute-start.12) | collective-permute-done | bytes 73760 | tf_op jit(solution)/shard_map/ppermute | solution.py:149
  91.6 2.1 %collective-permute-start.13 = (f32[72,256]{1,0:T(8,128)S(1)}, f32[72,256]{1,0:T(8,128)S(1)}, u32[]{:S(2)}, u32[]{:S(2)}) collective-permute-start(f32[72,256]{1,0:T(8,128)S(1)} %bitcast_add_fusion.11), channel_id=1, source_target_pairs={{4,8},{8,12},{12,14},{14,10},{10,6},{6,2},{2,0},{0,4},{5,9},{9,13}... | collective-permute-start | bytes 221192 | tf_op jit(solution)/shard_map/ppermute | solution.py:149
  94.4 1.6 %collective-permute-done.13 = f32[72,256]{1,0:T(8,128)S(1)} collective-permute-done((f32[72,256]{1,0:T(8,128)S(1)}, f32[72,256]{1,0:T(8,128)S(1)}, u32[]{:S(2)}, u32[]{:S(2)}) %collective-permute-start.13) | collective-permute-done | bytes 73760 | tf_op jit(solution)/shard_map/ppermute | solution.py:149
  96.0 2.1 %collective-permute-start.14 = (f32[72,256]{1,0:T(8,128)S(1)}, f32[72,256]{1,0:T(8,128)S(1)}, u32[]{:S(2)}, u32[]{:S(2)}) collective-permute-start(f32[72,256]{1,0:T(8,128)S(1)} %bitcast_add_fusion.10), channel_id=1, source_target_pairs={{4,8},{8,12},{12,14},{14,10},{10,6},{6,2},{2,0},{0,4},{5,9},{9,13}... | collective-permute-start | bytes 221192 | tf_op jit(solution)/shard_map/ppermute | solution.py:149
  98.8 1.9 %collective-permute-done.14 = f32[72,256]{1,0:T(8,128)S(1)} collective-permute-done((f32[72,256]{1,0:T(8,128)S(1)}, f32[72,256]{1,0:T(8,128)S(1)}, u32[]{:S(2)}, u32[]{:S(2)}) %collective-permute-start.14) | collective-permute-done | bytes 73760 | tf_op jit(solution)/shard_map/ppermute | solution.py:149
  100.7 2.5 %collective-permute-start.15 = (f32[72,256]{1,0:T(8,128)S(1)}, f32[72,256]{1,0:T(8,128)S(1)}, u32[]{:S(2)}, u32[]{:S(2)}) collective-permute-start(f32[72,256]{1,0:T(8,128)S(1)} %bitcast_add_fusion.9), channel_id=1, source_target_pairs={{4,8},{8,12},{12,14},{14,10},{10,6},{6,2},{2,0},{0,4},{5,9},{9,13}... | collective-permute-start | bytes 221192 | tf_op jit(solution)/shard_map/ppermute | solution.py:149
  105.3 2.4 %collective-permute-start.16 = (f32[72,256]{1,0:T(8,128)S(1)}, f32[72,256]{1,0:T(8,128)S(1)}, u32[]{:S(2)}, u32[]{:S(2)}) collective-permute-start(f32[72,256]{1,0:T(8,128)S(1)} %get-tuple-element.80), channel_id=1, source_target_pairs={{4,8},{8,12},{12,14},{14,10},{10,6},{6,2},{2,0},{0,4},{5,9},{9,13}... | collective-permute-start | bytes 221192 | tf_op jit(solution)/shard_map/ppermute | solution.py:168
  109.7 2.4 %collective-permute-start.17 = (f32[72,256]{1,0:T(8,128)S(1)}, f32[72,256]{1,0:T(8,128)S(1)}, u32[]{:S(2)}, u32[]{:S(2)}) collective-permute-start(f32[72,256]{1,0:T(8,128)S(1)} %collective-permute-done.16), channel_id=1, source_target_pairs={{4,8},{8,12},{12,14},{14,10},{10,6},{6,2},{2,0},{0,4},{5,9},{9,13}... | collective-permute-start | bytes 221192 | tf_op jit(solution)/shard_map/ppermute | solution.py:168
  112.6 2.0 %collective-permute-done.17 = f32[72,256]{1,0:T(8,128)S(1)} collective-permute-done((f32[72,256]{1,0:T(8,128)S(1)}, f32[72,256]{1,0:T(8,128)S(1)}, u32[]{:S(2)}, u32[]{:S(2)}) %collective-permute-start.17) | collective-permute-done | bytes 73760 | tf_op jit(solution)/shard_map/ppermute | solution.py:168
  114.6 2.5 %collective-permute-start.18 = (f32[72,256]{1,0:T(8,128)S(1)}, f32[72,256]{1,0:T(8,128)S(1)}, u32[]{:S(2)}, u32[]{:S(2)}) collective-permute-start(f32[72,256]{1,0:T(8,128)S(1)} %collective-permute-done.17), channel_id=1, source_target_pairs={{4,8},{8,12},{12,14},{14,10},{10,6},{6,2},{2,0},{0,4},{5,9},{9,13}... | collective-permute-start | bytes 221192 | tf_op jit(solution)/shard_map/ppermute | solution.py:168
  117.5 1.5 collective-permute-done.18
  119.0 2.4 %collective-permute-start.19 = (f32[72,256]{1,0:T(8,128)S(1)}, f32[72,256]{1,0:T(8,128)S(1)}, u32[]{:S(2)}, u32[]{:S(2)}) collective-permute-start(f32[72,256]{1,0:T(8,128)S(1)} %collective-permute-done.18), channel_id=1, source_target_pairs={{4,8},{8,12},{12,14},{14,10},{10,6},{6,2},{2,0},{0,4},{5,9},{9,13}... | collective-permute-start | bytes 221192 | tf_op jit(solution)/shard_map/ppermute | solution.py:168
  123.4 2.4 %collective-permute-start.20 = (f32[72,256]{1,0:T(8,128)S(1)}, f32[72,256]{1,0:T(8,128)S(1)}, u32[]{:S(2)}, u32[]{:S(2)}) collective-permute-start(f32[72,256]{1,0:T(8,128)S(1)} %collective-permute-done.19), channel_id=1, source_target_pairs={{4,8},{8,12},{12,14},{14,10},{10,6},{6,2},{2,0},{0,4},{5,9},{9,13}... | collective-permute-start | bytes 221192 | tf_op jit(solution)/shard_map/ppermute | solution.py:168
  127.8 2.4 %collective-permute-start.21 = (f32[72,256]{1,0:T(8,128)S(1)}, f32[72,256]{1,0:T(8,128)S(1)}, u32[]{:S(2)}, u32[]{:S(2)}) collective-permute-start(f32[72,256]{1,0:T(8,128)S(1)} %collective-permute-done.20), channel_id=1, source_target_pairs={{4,8},{8,12},{12,14},{14,10},{10,6},{6,2},{2,0},{0,4},{5,9},{9,13}... | collective-permute-start | bytes 221192 | tf_op jit(solution)/shard_map/ppermute | solution.py:168
  132.1 2.4 %collective-permute-start.22 = (f32[72,256]{1,0:T(8,128)S(1)}, f32[72,256]{1,0:T(8,128)S(1)}, u32[]{:S(2)}, u32[]{:S(2)}) collective-permute-start(f32[72,256]{1,0:T(8,128)S(1)} %collective-permute-done.21), channel_id=1, source_target_pairs={{4,8},{8,12},{12,14},{14,10},{10,6},{6,2},{2,0},{0,4},{5,9},{9,13}... | collective-permute-start | bytes 221192 | tf_op jit(solution)/shard_map/ppermute | solution.py:168
  136.5 2.8 %collective-permute-done.36 = f32[72,256]{1,0:T(8,128)S(1)} collective-permute-done((f32[72,256]{1,0:T(8,128)S(1)}, f32[72,256]{1,0:T(8,128)S(1)}, u32[]{:S(2)}, u32[]{:S(2)}) %collective-permute-start.36) | collective-permute-done | bytes 73760 | tf_op jit(solution)/shard_map/ppermute | solution.py:168
  141.4 5.6 %fusion.168 = bf16[16,32,256]{2,1,0:T(8,128)(2,1)} fusion(f32[22,35,256]{2,1,0:T(8,128)S(1)} %get-tuple-element.98, f32[16,32,256]{2,1,0:T(8,128)S(1)} %get-tuple-element.83, f32[3,32,256]{2,1,0:T(8,128)S(1)} %collective-permute-done.4, f32[22,35,256]{2,1,0:T(8,128)S(1)} %get-tuple-element.97, f32[3,32,256]{2,1,0:T(8,128)} %collective-permute-done.5, ...), kind=kLoop, calls=%fused_computation.379 | loop fusion | flops 13893632 | bytes 23315456 | tf_op jit(solution)/shard_map/convert_element_type | solution.py:275
  (317 shorter events, 51.2 us)
Async XLA Ops:
  1.6 10.6 %collective-permute-start = (bf16[3,32,256]{2,1,0:T(8,128)(2,1)S(1)}, bf16[3,32,256]{2,1,0:T(8,128)(2,1)S(1)}, u32[]{:S(2)}, u32[]{:S(2)}) collective-permute-start(bf16[3,32,256]{2,1,0:T(8,128)(2,1)S(1)} %get-tuple-element.109), channel_id=1, source_target_pairs={{0,2},{2,4},{4,6},{6,8},{8,10},{10,12},{12,14},{1,3},{3,5},{5,7},{... | collective-permute-start | bytes 147464 | tf_op jit(solution)/shard_map/ppermute | solution.py:17
  6.5 6.8 %collective-permute-start.1 = (bf16[3,32,256]{2,1,0:T(8,128)(2,1)S(1)}, bf16[3,32,256]{2,1,0:T(8,128)(2,1)S(1)}, u32[]{:S(2)}, u32[]{:S(2)}) collective-permute-start(bf16[3,32,256]{2,1,0:T(8,128)(2,1)S(1)} %get-tuple-element.108), channel_id=1, source_target_pairs={{2,0},{4,2},{6,4},{8,6},{10,8},{12,10},{14,12},{3,1},{5,3},{7,5},{... | collective-permute-start | bytes 147464 | tf_op jit(solution)/shard_map/ppermute | solution.py:20
  45.2 24.2 %collective-permute-start.8 = (f32[1152,256]{1,0:T(8,128)}, f32[1152,256]{1,0:T(8,128)}, u32[]{:S(2)}, u32[]{:S(2)}) collective-permute-start(f32[1152,256]{1,0:T(8,128)} %dynamic-slice_bitcast_fusion), channel_id=1, source_target_pairs={{0,1},{1,0},{2,3},{3,2},{4,5},{5,4},{6,7},{7,6},{8,9},{9,8},{10,11... | collective-permute-start | bytes 3538952 | tf_op jit(solution)/shard_map/ppermute | solution.py:149
  46.0 18.2 %collective-permute-start.4 = (f32[3,32,256]{2,1,0:T(8,128)}, f32[3,32,256]{2,1,0:T(8,128)S(1)}, u32[]{:S(2)}, u32[]{:S(2)}) collective-permute-start(f32[3,32,256]{2,1,0:T(8,128)} %get-tuple-element.101), channel_id=1, source_target_pairs={{0,2},{2,4},{4,6},{6,8},{8,10},{10,12},{12,14},{1,3},{3,5},{5,7},{... | collective-permute-start | bytes 294920 | tf_op jit(solution)/shard_map/ppermute | solution.py:17
  50.4 13.9 %collective-permute-start.5 = (f32[3,32,256]{2,1,0:T(8,128)}, f32[3,32,256]{2,1,0:T(8,128)}, u32[]{:S(2)}, u32[]{:S(2)}) collective-permute-start(f32[3,32,256]{2,1,0:T(8,128)} %get-tuple-element.102), channel_id=1, source_target_pairs={{2,0},{4,2},{6,4},{8,6},{10,8},{12,10},{14,12},{3,1},{5,3},{7,5},{... | collective-permute-start | bytes 294920 | tf_op jit(solution)/shard_map/ppermute | solution.py:20
  65.0 74.8 %collective-permute-start.6 = (f32[22,3,256]{2,1,0:T(4,128)S(1)}, f32[22,3,256]{2,1,0:T(4,128)S(1)}, u32[]{:S(2)}, u32[]{:S(2)}) collective-permute-start(f32[22,3,256]{2,1,0:T(4,128)S(1)} %get-tuple-element.99), channel_id=1, source_target_pairs={{1,0},{3,2},{5,4},{7,6},{9,8},{11,10},{13,12},{15,14},{17,16},{19,... | collective-permute-start | bytes 202760 | tf_op jit(solution)/shard_map/ppermute | solution.py:20
  66.3 73.5 %collective-permute-start.7 = (f32[22,3,256]{2,1,0:T(4,128)S(1)}, f32[22,3,256]{2,1,0:T(4,128)S(1)}, u32[]{:S(2)}, u32[]{:S(2)}) collective-permute-start(f32[22,3,256]{2,1,0:T(4,128)S(1)} %get-tuple-element.100), channel_id=1, source_target_pairs={{0,1},{2,3},{4,5},{6,7},{8,9},{10,11},{12,13},{14,15},{16,17},{18,... | collective-permute-start | bytes 202760 | tf_op jit(solution)/shard_map/ppermute | solution.py:17
  70.9 6.6 %collective-permute-start.9 = (f32[72,256]{1,0:T(8,128)S(1)}, f32[72,256]{1,0:T(8,128)S(1)}, u32[]{:S(2)}, u32[]{:S(2)}) collective-permute-start(f32[72,256]{1,0:T(8,128)S(1)} %dynamic-slice_bitcast_fusion.2), channel_id=1, source_target_pairs={{4,8},{8,12},{12,14},{14,10},{10,6},{6,2},{2,0},{0,4},{5,9},{9,13}... | collective-permute-start | bytes 221192 | tf_op jit(solution)/shard_map/ppermute | solution.py:149
  75.5 4.4 %collective-permute-start.23 = (f32[72,256]{1,0:T(8,128)S(1)}, f32[72,256]{1,0:T(8,128)S(1)}, u32[]{:S(2)}, u32[]{:S(2)}) collective-permute-start(f32[72,256]{1,0:T(8,128)S(1)} %dynamic-slice_bitcast_fusion.1), channel_id=1, source_target_pairs={{4,0},{8,4},{12,8},{14,12},{10,14},{6,10},{2,6},{0,2},{5,1},{9,5},... | collective-permute-start | bytes 221192 | tf_op jit(solution)/shard_map/ppermute | solution.py:149
  77.5 4.4 %collective-permute-start.10 = (f32[72,256]{1,0:T(8,128)S(1)}, f32[72,256]{1,0:T(8,128)S(1)}, u32[]{:S(2)}, u32[]{:S(2)}) collective-permute-start(f32[72,256]{1,0:T(8,128)S(1)} %bitcast_add_fusion.14), channel_id=1, source_target_pairs={{4,8},{8,12},{12,14},{14,10},{10,6},{6,2},{2,0},{0,4},{5,9},{9,13}... | collective-permute-start | bytes 221192 | tf_op jit(solution)/shard_map/ppermute | solution.py:149
  80.0 4.6 %collective-permute-start.24 = (f32[72,256]{1,0:T(8,128)S(1)}, f32[72,256]{1,0:T(8,128)S(1)}, u32[]{:S(2)}, u32[]{:S(2)}) collective-permute-start(f32[72,256]{1,0:T(8,128)S(1)} %bitcast_add_fusion.7), channel_id=1, source_target_pairs={{4,0},{8,4},{12,8},{14,12},{10,14},{6,10},{2,6},{0,2},{5,1},{9,5},... | collective-permute-start | bytes 221192 | tf_op jit(solution)/shard_map/ppermute | solution.py:149
  82.0 5.2 %collective-permute-start.11 = (f32[72,256]{1,0:T(8,128)S(1)}, f32[72,256]{1,0:T(8,128)S(1)}, u32[]{:S(2)}, u32[]{:S(2)}) collective-permute-start(f32[72,256]{1,0:T(8,128)S(1)} %bitcast_add_fusion.13), channel_id=1, source_target_pairs={{4,8},{8,12},{12,14},{14,10},{10,6},{6,2},{2,0},{0,4},{5,9},{9,13}... | collective-permute-start | bytes 221192 | tf_op jit(solution)/shard_map/ppermute | solution.py:149
  84.6 4.8 %collective-permute-start.25 = (f32[72,256]{1,0:T(8,128)S(1)}, f32[72,256]{1,0:T(8,128)S(1)}, u32[]{:S(2)}, u32[]{:S(2)}) collective-permute-start(f32[72,256]{1,0:T(8,128)S(1)} %bitcast_add_fusion.6), channel_id=1, source_target_pairs={{4,0},{8,4},{12,8},{14,12},{10,14},{6,10},{2,6},{0,2},{5,1},{9,5},... | collective-permute-start | bytes 221192 | tf_op jit(solution)/shard_map/ppermute | solution.py:149
  87.1 4.4 %collective-permute-start.12 = (f32[72,256]{1,0:T(8,128)S(1)}, f32[72,256]{1,0:T(8,128)S(1)}, u32[]{:S(2)}, u32[]{:S(2)}) collective-permute-start(f32[72,256]{1,0:T(8,128)S(1)} %bitcast_add_fusion.12), channel_id=1, source_target_pairs={{4,8},{8,12},{12,14},{14,10},{10,6},{6,2},{2,0},{0,4},{5,9},{9,13}... | collective-permute-start | bytes 221192 | tf_op jit(solution)/shard_map/ppermute | solution.py:149
  89.4 4.6 %collective-permute-start.26 = (f32[72,256]{1,0:T(8,128)S(1)}, f32[72,256]{1,0:T(8,128)S(1)}, u32[]{:S(2)}, u32[]{:S(2)}) collective-permute-start(f32[72,256]{1,0:T(8,128)S(1)} %bitcast_add_fusion.5), channel_id=1, source_target_pairs={{4,0},{8,4},{12,8},{14,12},{10,14},{6,10},{2,6},{0,2},{5,1},{9,5},... | collective-permute-start | bytes 221192 | tf_op jit(solution)/shard_map/ppermute | solution.py:149
  91.6 4.4 %collective-permute-start.13 = (f32[72,256]{1,0:T(8,128)S(1)}, f32[72,256]{1,0:T(8,128)S(1)}, u32[]{:S(2)}, u32[]{:S(2)}) collective-permute-start(f32[72,256]{1,0:T(8,128)S(1)} %bitcast_add_fusion.11), channel_id=1, source_target_pairs={{4,8},{8,12},{12,14},{14,10},{10,6},{6,2},{2,0},{0,4},{5,9},{9,13}... | collective-permute-start | bytes 221192 | tf_op jit(solution)/shard_map/ppermute | solution.py:149
  94.0 4.4 %collective-permute-start.27 = (f32[72,256]{1,0:T(8,128)S(1)}, f32[72,256]{1,0:T(8,128)S(1)}, u32[]{:S(2)}, u32[]{:S(2)}) collective-permute-start(f32[72,256]{1,0:T(8,128)S(1)} %bitcast_add_fusion.4), channel_id=1, source_target_pairs={{4,0},{8,4},{12,8},{14,12},{10,14},{6,10},{2,6},{0,2},{5,1},{9,5},... | collective-permute-start | bytes 221192 | tf_op jit(solution)/shard_map/ppermute | solution.py:149
  96.0 4.8 %collective-permute-start.14 = (f32[72,256]{1,0:T(8,128)S(1)}, f32[72,256]{1,0:T(8,128)S(1)}, u32[]{:S(2)}, u32[]{:S(2)}) collective-permute-start(f32[72,256]{1,0:T(8,128)S(1)} %bitcast_add_fusion.10), channel_id=1, source_target_pairs={{4,8},{8,12},{12,14},{14,10},{10,6},{6,2},{2,0},{0,4},{5,9},{9,13}... | collective-permute-start | bytes 221192 | tf_op jit(solution)/shard_map/ppermute | solution.py:149
  98.4 5.1 %collective-permute-start.28 = (f32[72,256]{1,0:T(8,128)S(1)}, f32[72,256]{1,0:T(8,128)S(1)}, u32[]{:S(2)}, u32[]{:S(2)}) collective-permute-start(f32[72,256]{1,0:T(8,128)S(1)} %bitcast_add_fusion.3), channel_id=1, source_target_pairs={{4,0},{8,4},{12,8},{14,12},{10,14},{6,10},{2,6},{0,2},{5,1},{9,5},... | collective-permute-start | bytes 221192 | tf_op jit(solution)/shard_map/ppermute | solution.py:149
  100.7 4.5 %collective-permute-start.15 = (f32[72,256]{1,0:T(8,128)S(1)}, f32[72,256]{1,0:T(8,128)S(1)}, u32[]{:S(2)}, u32[]{:S(2)}) collective-permute-start(f32[72,256]{1,0:T(8,128)S(1)} %bitcast_add_fusion.9), channel_id=1, source_target_pairs={{4,8},{8,12},{12,14},{14,10},{10,6},{6,2},{2,0},{0,4},{5,9},{9,13}... | collective-permute-start | bytes 221192 | tf_op jit(solution)/shard_map/ppermute | solution.py:149
  103.6 4.4 %collective-permute-start.29 = (f32[72,256]{1,0:T(8,128)S(1)}, f32[72,256]{1,0:T(8,128)S(1)}, u32[]{:S(2)}, u32[]{:S(2)}) collective-permute-start(f32[72,256]{1,0:T(8,128)S(1)} %bitcast_add_fusion.2), channel_id=1, source_target_pairs={{4,0},{8,4},{12,8},{14,12},{10,14},{6,10},{2,6},{0,2},{5,1},{9,5},... | collective-permute-start | bytes 221192 | tf_op jit(solution)/shard_map/ppermute | solution.py:149
  105.3 4.4 %collective-permute-start.16 = (f32[72,256]{1,0:T(8,128)S(1)}, f32[72,256]{1,0:T(8,128)S(1)}, u32[]{:S(2)}, u32[]{:S(2)}) collective-permute-start(f32[72,256]{1,0:T(8,128)S(1)} %get-tuple-element.80), channel_id=1, source_target_pairs={{4,8},{8,12},{12,14},{14,10},{10,6},{6,2},{2,0},{0,4},{5,9},{9,13}... | collective-permute-start | bytes 221192 | tf_op jit(solution)/shard_map/ppermute | solution.py:168
  108.1 4.4 %collective-permute-start.30 = (f32[72,256]{1,0:T(8,128)S(1)}, f32[72,256]{1,0:T(8,128)S(1)}, u32[]{:S(2)}, u32[]{:S(2)}) collective-permute-start(f32[72,256]{1,0:T(8,128)S(1)} %get-tuple-element.82), channel_id=1, source_target_pairs={{4,0},{8,4},{12,8},{14,12},{10,14},{6,10},{2,6},{0,2},{5,1},{9,5},... | collective-permute-start | bytes 221192 | tf_op jit(solution)/shard_map/ppermute | solution.py:168
  109.7 4.9 %collective-permute-start.17 = (f32[72,256]{1,0:T(8,128)S(1)}, f32[72,256]{1,0:T(8,128)S(1)}, u32[]{:S(2)}, u32[]{:S(2)}) collective-permute-start(f32[72,256]{1,0:T(8,128)S(1)} %collective-permute-done.16), channel_id=1, source_target_pairs={{4,8},{8,12},{12,14},{14,10},{10,6},{6,2},{2,0},{0,4},{5,9},{9,13}... | collective-permute-start | bytes 221192 | tf_op jit(solution)/shard_map/ppermute | solution.py:168
  112.5 5.0 %collective-permute-start.31 = (f32[72,256]{1,0:T(8,128)S(1)}, f32[72,256]{1,0:T(8,128)S(1)}, u32[]{:S(2)}, u32[]{:S(2)}) collective-permute-start(f32[72,256]{1,0:T(8,128)S(1)} %collective-permute-done.30), channel_id=1, source_target_pairs={{4,0},{8,4},{12,8},{14,12},{10,14},{6,10},{2,6},{0,2},{5,1},{9,5},... | collective-permute-start | bytes 221192 | tf_op jit(solution)/shard_map/ppermute | solution.py:168
  114.6 4.5 %collective-permute-start.18 = (f32[72,256]{1,0:T(8,128)S(1)}, f32[72,256]{1,0:T(8,128)S(1)}, u32[]{:S(2)}, u32[]{:S(2)}) collective-permute-start(f32[72,256]{1,0:T(8,128)S(1)} %collective-permute-done.17), channel_id=1, source_target_pairs={{4,8},{8,12},{12,14},{14,10},{10,6},{6,2},{2,0},{0,4},{5,9},{9,13}... | collective-permute-start | bytes 221192 | tf_op jit(solution)/shard_map/ppermute | solution.py:168
  117.5 4.4 %collective-permute-start.32 = (f32[72,256]{1,0:T(8,128)S(1)}, f32[72,256]{1,0:T(8,128)S(1)}, u32[]{:S(2)}, u32[]{:S(2)}) collective-permute-start(f32[72,256]{1,0:T(8,128)S(1)} %collective-permute-done.31), channel_id=1, source_target_pairs={{4,0},{8,4},{12,8},{14,12},{10,14},{6,10},{2,6},{0,2},{5,1},{9,5},... | collective-permute-start | bytes 221192 | tf_op jit(solution)/shard_map/ppermute | solution.py:168
  119.0 4.4 %collective-permute-start.19 = (f32[72,256]{1,0:T(8,128)S(1)}, f32[72,256]{1,0:T(8,128)S(1)}, u32[]{:S(2)}, u32[]{:S(2)}) collective-permute-start(f32[72,256]{1,0:T(8,128)S(1)} %collective-permute-done.18), channel_id=1, source_target_pairs={{4,8},{8,12},{12,14},{14,10},{10,6},{6,2},{2,0},{0,4},{5,9},{9,13}... | collective-permute-start | bytes 221192 | tf_op jit(solution)/shard_map/ppermute | solution.py:168
  121.9 4.4 %collective-permute-start.33 = (f32[72,256]{1,0:T(8,128)S(1)}, f32[72,256]{1,0:T(8,128)S(1)}, u32[]{:S(2)}, u32[]{:S(2)}) collective-permute-start(f32[72,256]{1,0:T(8,128)S(1)} %collective-permute-done.32), channel_id=1, source_target_pairs={{4,0},{8,4},{12,8},{14,12},{10,14},{6,10},{2,6},{0,2},{5,1},{9,5},... | collective-permute-start | bytes 221192 | tf_op jit(solution)/shard_map/ppermute | solution.py:168
  126.2 4.4 %collective-permute-start.34 = (f32[72,256]{1,0:T(8,128)S(1)}, f32[72,256]{1,0:T(8,128)S(1)}, u32[]{:S(2)}, u32[]{:S(2)}) collective-permute-start(f32[72,256]{1,0:T(8,128)S(1)} %collective-permute-done.33), channel_id=1, source_target_pairs={{4,0},{8,4},{12,8},{14,12},{10,14},{6,10},{2,6},{0,2},{5,1},{9,5},... | collective-permute-start | bytes 221192 | tf_op jit(solution)/shard_map/ppermute | solution.py:168
  127.8 4.4 %collective-permute-start.21 = (f32[72,256]{1,0:T(8,128)S(1)}, f32[72,256]{1,0:T(8,128)S(1)}, u32[]{:S(2)}, u32[]{:S(2)}) collective-permute-start(f32[72,256]{1,0:T(8,128)S(1)} %collective-permute-done.20), channel_id=1, source_target_pairs={{4,8},{8,12},{12,14},{14,10},{10,6},{6,2},{2,0},{0,4},{5,9},{9,13}... | collective-permute-start | bytes 221192 | tf_op jit(solution)/shard_map/ppermute | solution.py:168
  139.8 7.4 %collective-permute-start.37 = (f32[1152,256]{1,0:T(8,128)S(1)}, f32[1152,256]{1,0:T(8,128)S(1)}, u32[]{:S(2)}, u32[]{:S(2)}) collective-permute-start(f32[1152,256]{1,0:T(8,128)S(1)} %bitcast.224), channel_id=1, source_target_pairs={{0,1},{1,0},{2,3},{3,2},{4,5},{5,4},{6,7},{7,6},{8,9},{9,8},{10,11... | collective-permute-start | bytes 3538952 | tf_op jit(solution)/shard_map/ppermute | solution.py:168
  (100 other events, 742.9 us)

commit v2 on v1

--- a/solution.py
+++ b/solution.py
@@ -172,11 +172,48 @@
     return stacked.reshape(-1, stacked.shape[-1])
 
 
+def halving_stages(sizes):
+    stages = []
+    for axis, count in sizes:
+        bit = 1
+        while bit < count:
+            stages.append((axis, count, bit))
+            bit *= 2
+    return stages
+
+
+def stage_side(axis, bit):
+    return (lax.axis_index(axis) // bit) % 2
+
+
+def stage_pairs(count, bit):
+    return [(i, i ^ bit) for i in range(count)]
+
+
+def halving_reduce_scatter(block, stages):
+    for axis, count, bit in stages:
+        half = block.shape[0] // 2
+        side = stage_side(axis, bit)
+        kept = lax.dynamic_slice_in_dim(block, side * half, half, axis=0)
+        sent = lax.dynamic_slice_in_dim(block, (1 - side) * half, half, axis=0)
+        block = kept + lax.ppermute(sent, axis, stage_pairs(count, bit))
+    return block
+
+
+def doubling_all_gather(block, stages):
+    for axis, count, bit in reversed(stages):
+        side = stage_side(axis, bit)
+        other = lax.ppermute(block, axis, stage_pairs(count, bit))
+        full = jnp.zeros((2 * block.shape[0],) + block.shape[1:], block.dtype)
+        full = lax.dynamic_update_slice_in_dim(full, block, side * block.shape[0], axis=0)
+        block = lax.dynamic_update_slice_in_dim(full, other, (1 - side) * block.shape[0], axis=0)
+    return block
+
+
 def ring_all_reduce(block, row_order, col_order):
-    block = ring_reduce_scatter(block, "col", col_order, 1)[0]
-    held = ring_reduce_scatter(block, "row", row_order, 2)
-    block = ring_all_gather(held, "row", row_order)
-    return ring_all_gather([block], "col", col_order)
+    stages = halving_stages((("col", len(col_order)), ("row", len(row_order))))
+    block = halving_reduce_scatter(block, stages)
+    return doubling_all_gather(block.astype(jnp.bfloat16), stages).astype(jnp.float32)
 
 
 def per_device(

time: 153 us -> 128 us (0.84)
  starting transfers between devices: 56.7 us -> 33.9 us
  between operations: 13.8 us -> 2.13 us
  waiting for transfers between devices: 31.3 us -> 39.2 us
    ppermute x30 -> x8, starting transfers between devices: 37.9 us -> 16.7 us  [the longest x4 8.43 us: doubling_all_gather(): other = lax.ppermute(block, axis, stage_pairs(count, bit))]
    ppermute x30 -> x8, waiting for transfers between devices: 30.1 us -> 37.1 us  [the longest x4 28.9 us: halving_reduce_scatter(): block = kept + lax.ppermute(sent, axis, stage_pairs(count, bit))]
    add x13 -> x3, other arithmetic: 1.55 us -> 3.65 us  [halving_reduce_scatter(): block = kept + lax.ppermute(sent, axis, stage_pairs(count, bit))]
    ppermute x4, starting transfers between devices: 13.7 us -> 12 us  [with_halo(): lax.ppermute(lax.slice_in_dim(block, block.shape[dim] - width, None, axis...]
  transfers between devices with their start and end apart: 38 -> 16, of which waited for: 28 -> 8; matrix products, arithmetic and copies ran while one was open for 11% -> 9% of each run, Pallas kernels for 0% -> 0%
where the time goes in v2:
time: 128 us; the launch traced here: 127 us
  waiting for transfers between devices  39.2 us (31%)
  starting transfers between devices  33.9 us (26%)
  other arithmetic  24.4 us (19%)
  local copies, waits for them, and re-layouts  17.5 us (14%)
  matrix products  9.51 us (7%)
  between operations  2.13 us (2%)
    ppermute x4, waiting for transfers between devices, halving_reduce_scatter(): block = kept + lax.ppermute(sent, axis, stage_pairs(count, bit))  28.9 us
    ppermute x4, starting transfers between devices, with_halo(): lax.ppermute(lax.slice_in_dim(block, block.shape[dim] - width, None, axis...  12 us
    ppermute x4, starting transfers between devices, doubling_all_gather(): other = lax.ppermute(block, axis, stage_pairs(count, bit))  8.43 us
    ppermute x4, starting transfers between devices, halving_reduce_scatter(): block = kept + lax.ppermute(sent, axis, stage_pairs(count, bit))  8.27 us
    ppermute x4, waiting for transfers between devices, doubling_all_gather(): other = lax.ppermute(block, axis, stage_pairs(count, bit))  8.18 us
    concatenate x1, local copies, waits for them, and re-layouts, per_device(): jnp.concatenate(flat, axis=0)  6.61 us
    reduce_sum x1, other arithmetic, forward_back(): centred = conv_out - jnp.mean(conv_out, axis=2, keepdims=True)  5.63 us
    ppermute x4, starting transfers between devices, with_halo(): lax.ppermute(lax.slice_in_dim(block, 0, width, axis=dim), axis, backward)  5.17 us
  transfers between devices with their start and end apart: 16, of which 8 were waited for; matrix products, arithmetic and copies ran while one was open for 9% of the time, Pallas kernels for 0%

profile of v2, /device:TPU:0, one launch (start us, length us, event | category | flops | bytes accessed | tf_op | source)
XLA Modules:
  0.0 126.7 jit_solution(17096660276885256789)
XLA Ops:
  1.6 4.9 %collective-permute-start = (bf16[3,32,256]{2,1,0:T(8,128)(2,1)S(1)}, bf16[3,32,256]{2,1,0:T(8,128)(2,1)S(1)}, u32[]{:S(2)}, u32[]{:S(2)}) collective-permute-start(bf16[3,32,256]{2,1,0:T(8,128)(2,1)S(1)} %get-tuple-element.105), channel_id=1, source_target_pairs={{0,2},{2,4},{4,6},{6,8},{8,10},{10,12},{12,14},{1,3},{3,5},{5,7},{... | collective-permute-start | bytes 147464 | tf_op jit(solution)/shard_map/ppermute | solution.py:17
  6.5 1.3 %collective-permute-start.1 = (bf16[3,32,256]{2,1,0:T(8,128)(2,1)S(1)}, bf16[3,32,256]{2,1,0:T(8,128)(2,1)S(1)}, u32[]{:S(2)}, u32[]{:S(2)}) collective-permute-start(bf16[3,32,256]{2,1,0:T(8,128)(2,1)S(1)} %get-tuple-element.104), channel_id=1, source_target_pairs={{2,0},{4,2},{6,4},{8,6},{10,8},{12,10},{14,12},{3,1},{5,3},{7,5},{... | collective-permute-start | bytes 147464 | tf_op jit(solution)/shard_map/ppermute | solution.py:20
  13.3 1.5 %collective-permute-start.2 = (bf16[22,3,256]{2,1,0:T(4,128)(2,1)S(1)}, bf16[22,3,256]{2,1,0:T(4,128)(2,1)S(1)}, u32[]{:S(2)}, u32[]{:S(2)}) collective-permute-start(bf16[22,3,256]{2,1,0:T(4,128)(2,1)S(1)} %get-tuple-element.99), channel_id=1, source_target_pairs={{0,1},{2,3},{4,5},{6,7},{8,9},{10,11},{12,13},{14,15},{16,17},{18,... | collective-permute-start | bytes 101384 | tf_op jit(solution)/shard_map/ppermute | solution.py:17
  14.8 1.3 %collective-permute-start.3 = (bf16[22,3,256]{2,1,0:T(4,128)(2,1)S(1)}, bf16[22,3,256]{2,1,0:T(4,128)(2,1)S(1)}, u32[]{:S(2)}, u32[]{:S(2)}) collective-permute-start(bf16[22,3,256]{2,1,0:T(4,128)(2,1)S(1)} %get-tuple-element.100), channel_id=1, source_target_pairs={{1,0},{3,2},{5,4},{7,6},{9,8},{11,10},{13,12},{15,14},{17,16},{19,... | collective-permute-start | bytes 101384 | tf_op jit(solution)/shard_map/ppermute | solution.py:20
  17.9 5.6 %fusion.211 = (f32[16,32]{1,0:T(8,128)S(1)}, f32[16,32,256]{2,1,0:T(8,128)S(1)}) fusion(f32[256]{0:T(256)S(1)} %copy-done.76, f32[256]{0:T(256)S(1)} %bitcast.236, bf16[22,3,256]{2,1,0:T(4,128)(2,1)S(1)} %collective-permute-done.3, bf16[22,32,256]{2,1,0:T(8,128)(2,1)S(1)} %get-tuple-element.158, f32[256]{0:T(256)S(1)} %bitcast.238, f32[256]{0:T(256)S(1)} %bitcast.144, ...), kind=kLoop, calls=%fused_computation.498 | loop fusion | flops 35913216 | bytes 2840576 | tf_op jit(solution)/shard_map/reduce_sum | solution.py:59
  25.0 1.6 %multiply_convert_fusion = (bf16[512,1024]{1,0:T(8,128)(2,1)}, f32[512,1024]{1,0:T(8,128)S(1)}) fusion(f32[1024]{0:T(1024)S(1)} %copy-done.65, bf16[512,256]{1,0:T(8,128)(2,1)S(1)} %bitcast.140, bf16[256,1024]{1,0:T(8,128)(2,1)S(1)} %copy-done), kind=kOutput, calls=%fused_computation.48 | convolution fusion | flops 271581184 | bytes 3936256 | tf_op jit(solution)/shard_map/dot_general | solution.py:63
  26.6 1.9 %convert_reduce_fusion = (f32[1024]{0:T(1024)}, bf16[512,1024]{1,0:T(8,128)(2,1)S(1)}) fusion(f32[512,1024]{1,0:T(8,128)S(1)} %get-tuple-element.161, f32[1024]{0:T(1024)S(1)} %copy-done.65, bf16[512,256]{1,0:T(8,128)(2,1)S(1)} %fusion.166, bf16[1024,256]{1,0:T(8,128)(2,1)S(1)} %copy-done.77), kind=kOutput, calls=%fused_computation.47 | convolution fusion | flops 275250176 | bytes 3940352 | tf_op jit(solution)/shard_map/dot_general | solution.py:70
  28.5 1.5 %fusion.219 = f32[1024,256]{1,0:T(8,128)} fusion(bf16[512,1024]{1,0:T(8,128)(2,1)S(1)} %get-tuple-element.163, bf16[512,256]{1,0:T(8,128)(2,1)S(1)} %bitcast.141), kind=kOutput, calls=%fused_computation.505 | convolution fusion | flops 268435456 | bytes 2359296 | tf_op jit(solution)/shard_map/dot_general | solution.py:252
  31.3 1.7 %fusion.159 = (f32[256]{0:T(256)S(1)}, f32[256]{0:T(256)}, f32[256]{0:T(256)}, f32[256]{0:T(256)}, f32[256]{0:T(256)}, /*index=5*/f32[256]{0:T(256)}, f32[256]{0...) fusion(bf16[22,3,256]{2,1,0:T(4,128)(2,1)S(1)} %collective-permute-done.3, ...), kind=kLoop, calls=%fused_computation.316 | loop fusion | flops 7730944 | bytes 1983488 | tf_op jit(solution)/shard_map/reduce_sum | solution.py:268
  36.4 1.4 %fusion.220 = f32[1024,256]{1,0:T(8,128)} fusion(bf16[512,1024]{1,0:T(8,128)(2,1)S(1)} %copy-done.1, bf16[512,256]{1,0:T(8,128)(2,1)S(1)} %copy-done.7), kind=kOutput, calls=%fused_computation.506 | convolution fusion | flops 268435456 | bytes 2359296 | tf_op jit(solution)/shard_map/dot_general | solution.py:256
  37.8 2.1 %fusion.7 = f32[256]{0:T(256)} fusion(bf16[512,1024]{1,0:T(8,128)(2,1)S(1)} %copy-done.1, bf16[1024,256]{1,0:T(8,128)(2,1)} %param.19, f32[256]{0:T(256)S(1)} %copy-done.78, bf16[512,256]{1,0:T(8,128)(2,1)S(1)} %bitcast.139), kind=kOutput, calls=%fused_computation.53 | convolution fusion | flops 268959488 | bytes 1837056 | tf_op jit(solution)/shard_map/dot_general | solution.py:66
  40.6 6.6 %concatenate.133 = f32[2304,256]{1,0:T(8,128)S(1)} concatenate(f32[1024,256]{1,0:T(8,128)} %fusion.219, f32[1024,256]{1,0:T(8,128)} %fusion.220, f32[49,256]{1,0:T(8,128)S(1)} %stack.199, f32[1,256]{1,0:T(1,128)} %bitcast.293, f32[1,256]{1,0:T(1,128)} %bitcast.292, f32[1,256]{1,0:T(1,128)} %bitcast.291, f32[4,256]{1,0:T(4,128)S(1)} %reshape.159, f32[1,256]{1,0:T(1,128)} %bitcast.290, ...), dimensions={0} | concatenate | bytes 4718592 | tf_op jit(solution)/shard_map/concatenate | solution.py:300
  47.2 1.1 constant_dynamic-slice_fusion.3
  48.5 3.1 %collective-permute-done.8 = f32[1152,256]{1,0:T(8,128)} collective-permute-done((f32[1152,256]{1,0:T(8,128)}, f32[1152,256]{1,0:T(8,128)}, u32[]{:S(2)}, u32[]{:S(2)}) %collective-permute-start.8) | collective-permute-done | bytes 1179680 | tf_op jit(solution)/shard_map/ppermute | solution.py:199
  51.5 2.5 %dynamic-slice_add_fusion = f32[1152,256]{1,0:T(8,128)} fusion(f32[1152,256]{1,0:T(8,128)} %collective-permute-done.8, f32[2304,256]{1,0:T(8,128)S(1)} %concatenate.133, s32[]{:T(128)S(6)} %select_n.73), kind=kLoop, calls=%fused_computation.52 | loop fusion | flops 294912 | bytes 3538948 | tf_op jit(solution)/shard_map/add | solution.py:199
  55.1 2.5 %collective-permute-start.9 = (f32[576,256]{1,0:T(8,128)S(1)}, f32[576,256]{1,0:T(8,128)S(1)}, u32[]{:S(2)}, u32[]{:S(2)}) collective-permute-start(f32[576,256]{1,0:T(8,128)S(1)} %constant_dynamic-slice_fusion.2), channel_id=1, source_target_pairs={{0,2},{2,0},{4,6},{6,4},{8,10},{10,8},{12,14},{14,12},{1,3},{3,1},... | collective-permute-start | bytes 1769480 | tf_op jit(solution)/shard_map/ppermute | solution.py:199
  57.6 13.6 %collective-permute-done.9 = f32[576,256]{1,0:T(8,128)S(1)} collective-permute-done((f32[576,256]{1,0:T(8,128)S(1)}, f32[576,256]{1,0:T(8,128)S(1)}, u32[]{:S(2)}, u32[]{:S(2)}) %collective-permute-start.9) | collective-permute-done | bytes 589856 | tf_op jit(solution)/shard_map/ppermute | solution.py:199
  71.3 1.1 dynamic-slice_add_fusion.1
  72.5 2.8 %collective-permute-start.10 = (f32[288,256]{1,0:T(8,128)S(1)}, f32[288,256]{1,0:T(8,128)S(1)}, u32[]{:S(2)}, u32[]{:S(2)}) collective-permute-start(f32[288,256]{1,0:T(8,128)S(1)} %constant_dynamic-slice_fusion.1), channel_id=1, source_target_pairs={{0,4},{2,6},{4,0},{6,2},{8,12},{10,14},{12,8},{14,10},{1,5},{3,7},... | collective-permute-start | bytes 884744 | tf_op jit(solution)/shard_map/ppermute | solution.py:199
  75.3 6.5 %collective-permute-done.10 = f32[288,256]{1,0:T(8,128)S(1)} collective-permute-done((f32[288,256]{1,0:T(8,128)S(1)}, f32[288,256]{1,0:T(8,128)S(1)}, u32[]{:S(2)}, u32[]{:S(2)}) %collective-permute-start.10) | collective-permute-done | bytes 294944 | tf_op jit(solution)/shard_map/ppermute | solution.py:199
  81.8 2.8 %collective-permute-start.11 = (f32[144,256]{1,0:T(8,128)S(1)}, f32[144,256]{1,0:T(8,128)S(1)}, u32[]{:S(2)}, u32[]{:S(2)}) collective-permute-start(f32[144,256]{1,0:T(8,128)S(1)} %constant_dynamic-slice_fusion), channel_id=1, source_target_pairs={{0,8},{2,10},{4,12},{6,14},{8,0},{10,2},{12,4},{14,6},{1,9},{3,11}... | collective-permute-start | bytes 442376 | tf_op jit(solution)/shard_map/ppermute | solution.py:199
  84.6 5.8 %collective-permute-done.11 = f32[144,256]{1,0:T(8,128)S(1)} collective-permute-done((f32[144,256]{1,0:T(8,128)S(1)}, f32[144,256]{1,0:T(8,128)S(1)}, u32[]{:S(2)}, u32[]{:S(2)}) %collective-permute-start.11) | collective-permute-done | bytes 147488 | tf_op jit(solution)/shard_map/ppermute | solution.py:199
  90.9 2.5 %collective-permute-start.4 = (f32[3,32,256]{2,1,0:T(8,128)S(1)}, f32[3,32,256]{2,1,0:T(8,128)S(1)}, u32[]{:S(2)}, u32[]{:S(2)}) collective-permute-start(f32[3,32,256]{2,1,0:T(8,128)S(1)} %get-tuple-element.97), channel_id=1, source_target_pairs={{0,2},{2,4},{4,6},{6,8},{8,10},{10,12},{12,14},{1,3},{3,5},{5,7},{... | collective-permute-start | bytes 294920 | tf_op jit(solution)/shard_map/ppermute | solution.py:17
  93.4 1.3 %collective-permute-start.5 = (f32[3,32,256]{2,1,0:T(8,128)S(1)}, f32[3,32,256]{2,1,0:T(8,128)S(1)}, u32[]{:S(2)}, u32[]{:S(2)}) collective-permute-start(f32[3,32,256]{2,1,0:T(8,128)S(1)} %get-tuple-element.98), channel_id=1, source_target_pairs={{2,0},{4,2},{6,4},{8,6},{10,8},{12,10},{14,12},{3,1},{5,3},{7,5},{... | collective-permute-start | bytes 294920 | tf_op jit(solution)/shard_map/ppermute | solution.py:20
  94.7 1.9 %collective-permute-done.12 = bf16[144,256]{1,0:T(8,128)(2,1)S(1)} collective-permute-done((bf16[144,256]{1,0:T(8,128)(2,1)S(1)}, bf16[144,256]{1,0:T(8,128)(2,1)S(1)}, u32[]{:S(2)}, u32[]{:S(2)}) %collective-permute-start.12) | collective-permute-done | bytes 73760 | tf_op jit(solution)/shard_map/ppermute | solution.py:206
  96.5 4.8 %collective-permute-start.13 = (bf16[288,256]{1,0:T(8,128)(2,1)S(1)}, bf16[288,256]{1,0:T(8,128)(2,1)S(1)}, u32[]{:S(2)}, u32[]{:S(2)}) collective-permute-start(bf16[288,256]{1,0:T(8,128)(2,1)S(1)} %constant_dynamic-update-slice_fusion.13), channel_id=1, source_target_pairs={{0,4},{2,6},{4,0},{6,2},{8,12},{10,14},{12,8},{14,10},{1,5},{3,7},... | collective-permute-start | bytes 442376 | tf_op jit(solution)/shard_map/ppermute | solution.py:206
  102.3 1.3 %collective-permute-start.6 = (f32[22,3,256]{2,1,0:T(4,128)S(1)}, f32[22,3,256]{2,1,0:T(4,128)S(1)}, u32[]{:S(2)}, u32[]{:S(2)}) collective-permute-start(f32[22,3,256]{2,1,0:T(4,128)S(1)} %get-tuple-element.95), channel_id=1, source_target_pairs={{1,0},{3,2},{5,4},{7,6},{9,8},{11,10},{13,12},{15,14},{17,16},{19,... | collective-permute-start | bytes 202760 | tf_op jit(solution)/shard_map/ppermute | solution.py:20
  103.6 3.2 %collective-permute-start.7 = (f32[22,3,256]{2,1,0:T(4,128)S(1)}, f32[22,3,256]{2,1,0:T(4,128)S(1)}, u32[]{:S(2)}, u32[]{:S(2)}) collective-permute-start(f32[22,3,256]{2,1,0:T(4,128)S(1)} %get-tuple-element.96), channel_id=1, source_target_pairs={{0,1},{2,3},{4,5},{6,7},{8,9},{10,11},{12,13},{14,15},{16,17},{18,... | collective-permute-start | bytes 202760 | tf_op jit(solution)/shard_map/ppermute | solution.py:17
  107.3 3.2 %collective-permute-start.14 = (bf16[576,256]{1,0:T(8,128)(2,1)S(1)}, bf16[576,256]{1,0:T(8,128)(2,1)S(1)}, u32[]{:S(2)}, u32[]{:S(2)}) collective-permute-start(bf16[576,256]{1,0:T(8,128)(2,1)S(1)} %constant_dynamic-update-slice_fusion.11), channel_id=1, source_target_pairs={{0,2},{2,0},{4,6},{6,4},{8,10},{10,8},{12,14},{14,12},{1,3},{3,1},... | collective-permute-start | bytes 884744 | tf_op jit(solution)/shard_map/ppermute | solution.py:206
  110.6 6.3 %collective-permute-done.14 = bf16[576,256]{1,0:T(8,128)(2,1)S(1)} collective-permute-done((bf16[576,256]{1,0:T(8,128)(2,1)S(1)}, bf16[576,256]{1,0:T(8,128)(2,1)S(1)}, u32[]{:S(2)}, u32[]{:S(2)}) %collective-permute-start.14) | collective-permute-done | bytes 294944 | tf_op jit(solution)/shard_map/ppermute | solution.py:206
  117.4 4.7 %fusion.168 = bf16[16,32,256]{2,1,0:T(8,128)(2,1)} fusion(f32[22,35,256]{2,1,0:T(8,128)S(1)} %get-tuple-element.94, f32[16,32,256]{2,1,0:T(8,128)S(1)} %get-tuple-element.81, f32[3,32,256]{2,1,0:T(8,128)S(1)} %collective-permute-done.4, f32[22,35,256]{2,1,0:T(8,128)S(1)} %get-tuple-element.93, f32[3,32,256]{2,1,0:T(8,128)S(1)} %collective-permute-done.5, ...), kind=kLoop, calls=%fused_computation.377 | loop fusion | flops 13893632 | bytes 23315456 | tf_op jit(solution)/shard_map/convert_element_type | solution.py:312
  124.8 1.3 %copy.21 = f32[256,1024]{1,0:T(8,128)} copy(f32[256,1024]{0,1:T(8,128)S(1)} %get-tuple-element.92) | data formatting | bytes 2097152
  (223 shorter events, 21.1 us)
Async XLA Ops:
  0.6 24.4 %copy-start = (bf16[256,1024]{1,0:T(8,128)(2,1)S(1)}, bf16[256,1024]{1,0:T(8,128)(2,1)}, u32[]{:S(2)}) copy-start(bf16[256,1024]{1,0:T(8,128)(2,1)} %param.17) | copy-start | bytes 1572868
  0.7 17.2 %copy-start.2 = (bf16[16,32,256]{2,1,0:T(8,128)(2,1)S(1)}, bf16[16,32,256]{2,1,0:T(8,128)(2,1)}, u32[]{:S(2)}) copy-start(bf16[16,32,256]{2,1,0:T(8,128)(2,1)} %param.11) | copy-start | bytes 786436
  0.7 15.4 %copy-start.3 = (bf16[16,32,256]{2,1,0:T(8,128)(2,1)S(1)}, bf16[16,32,256]{2,1,0:T(8,128)(2,1)}, u32[]{:S(2)}) copy-start(bf16[16,32,256]{2,1,0:T(8,128)(2,1)} %param.12) | copy-start | bytes 786436
  0.7 15.4 %copy-start.66 = (f32[256]{0:T(256)S(1)}, f32[256]{0:T(256)}, u32[]{:S(2)}) copy-start(f32[256]{0:T(256)} %param.21) | copy-start | bytes 3076
  0.7 17.2 %copy-start.76 = (f32[256]{0:T(256)S(1)}, f32[256]{0:T(256)}, u32[]{:S(2)}) copy-start(f32[256]{0:T(256)} %param.14) | copy-start | bytes 3076
  1.6 10.5 %collective-permute-start = (bf16[3,32,256]{2,1,0:T(8,128)(2,1)S(1)}, bf16[3,32,256]{2,1,0:T(8,128)(2,1)S(1)}, u32[]{:S(2)}, u32[]{:S(2)}) collective-permute-start(bf16[3,32,256]{2,1,0:T(8,128)(2,1)S(1)} %get-tuple-element.105), channel_id=1, source_target_pairs={{0,2},{2,4},{4,6},{6,8},{8,10},{10,12},{12,14},{1,3},{3,5},{5,7},{... | collective-permute-start | bytes 147464 | tf_op jit(solution)/shard_map/ppermute | solution.py:17
  6.5 6.7 %collective-permute-start.1 = (bf16[3,32,256]{2,1,0:T(8,128)(2,1)S(1)}, bf16[3,32,256]{2,1,0:T(8,128)(2,1)S(1)}, u32[]{:S(2)}, u32[]{:S(2)}) collective-permute-start(bf16[3,32,256]{2,1,0:T(8,128)(2,1)S(1)} %get-tuple-element.104), channel_id=1, source_target_pairs={{2,0},{4,2},{6,4},{8,6},{10,8},{12,10},{14,12},{3,1},{5,3},{7,5},{... | collective-permute-start | bytes 147464 | tf_op jit(solution)/shard_map/ppermute | solution.py:20
  9.9 13.6 %copy-start.9 = (f32[1,256]{1,0:T(1,128)}, f32[1,256]{1,0:T(1,128)S(1)}, u32[]{:S(2)}) copy-start(f32[1,256]{1,0:T(1,128)S(1)} %get-tuple-element.127) | copy-start | bytes 3076
  9.9 13.6 %copy-start.11 = (f32[1,256]{1,0:T(1,128)}, f32[1,256]{1,0:T(1,128)S(1)}, u32[]{:S(2)}) copy-start(f32[1,256]{1,0:T(1,128)S(1)} %get-tuple-element.128) | copy-start | bytes 3076
  9.9 13.6 %copy-start.13 = (f32[1,256]{1,0:T(1,128)}, f32[1,256]{1,0:T(1,128)S(1)}, u32[]{:S(2)}) copy-start(f32[1,256]{1,0:T(1,128)S(1)} %get-tuple-element.129) | copy-start | bytes 3076
  9.9 13.6 %copy-start.15 = (f32[1,256]{1,0:T(1,128)}, f32[1,256]{1,0:T(1,128)S(1)}, u32[]{:S(2)}) copy-start(f32[1,256]{1,0:T(1,128)S(1)} %get-tuple-element.130) | copy-start | bytes 3076
  9.9 13.6 %copy-start.17 = (f32[1,256]{1,0:T(1,128)}, f32[1,256]{1,0:T(1,128)S(1)}, u32[]{:S(2)}) copy-start(f32[1,256]{1,0:T(1,128)S(1)} %get-tuple-element.131) | copy-start | bytes 3076
  9.9 13.6 %copy-start.19 = (f32[1,256]{1,0:T(1,128)}, f32[1,256]{1,0:T(1,128)S(1)}, u32[]{:S(2)}) copy-start(f32[1,256]{1,0:T(1,128)S(1)} %get-tuple-element.132) | copy-start | bytes 3076
  10.0 13.6 %copy-start.21 = (f32[1,256]{1,0:T(1,128)}, f32[1,256]{1,0:T(1,128)S(1)}, u32[]{:S(2)}) copy-start(f32[1,256]{1,0:T(1,128)S(1)} %get-tuple-element.133) | copy-start | bytes 3076
  10.0 13.6 %copy-start.23 = (f32[1,256]{1,0:T(1,128)}, f32[1,256]{1,0:T(1,128)S(1)}, u32[]{:S(2)}) copy-start(f32[1,256]{1,0:T(1,128)S(1)} %get-tuple-element.134) | copy-start | bytes 3076
  10.0 13.6 %copy-start.25 = (f32[1,256]{1,0:T(1,128)}, f32[1,256]{1,0:T(1,128)S(1)}, u32[]{:S(2)}) copy-start(f32[1,256]{1,0:T(1,128)S(1)} %get-tuple-element.135) | copy-start | bytes 3076
  10.0 13.6 %copy-start.27 = (f32[1,256]{1,0:T(1,128)}, f32[1,256]{1,0:T(1,128)S(1)}, u32[]{:S(2)}) copy-start(f32[1,256]{1,0:T(1,128)S(1)} %get-tuple-element.136) | copy-start | bytes 3076
  11.1 15.5 %copy-start.6 = (bf16[512,256]{1,0:T(8,128)(2,1)}, bf16[512,256]{1,0:T(8,128)(2,1)S(1)}, u32[]{:S(2)}) copy-start(bf16[512,256]{1,0:T(8,128)(2,1)S(1)} %fusion.166) | copy-start | bytes 786436
  13.3 3.5 %collective-permute-start.2 = (bf16[22,3,256]{2,1,0:T(4,128)(2,1)S(1)}, bf16[22,3,256]{2,1,0:T(4,128)(2,1)S(1)}, u32[]{:S(2)}, u32[]{:S(2)}) collective-permute-start(bf16[22,3,256]{2,1,0:T(4,128)(2,1)S(1)} %get-tuple-element.99), channel_id=1, source_target_pairs={{0,1},{2,3},{4,5},{6,7},{8,9},{10,11},{12,13},{14,15},{16,17},{18,... | collective-permute-start | bytes 101384 | tf_op jit(solution)/shard_map/ppermute | solution.py:17
  14.8 3.1 %collective-permute-start.3 = (bf16[22,3,256]{2,1,0:T(4,128)(2,1)S(1)}, bf16[22,3,256]{2,1,0:T(4,128)(2,1)S(1)}, u32[]{:S(2)}, u32[]{:S(2)}) collective-permute-start(bf16[22,3,256]{2,1,0:T(4,128)(2,1)S(1)} %get-tuple-element.100), channel_id=1, source_target_pairs={{1,0},{3,2},{5,4},{7,6},{9,8},{11,10},{13,12},{15,14},{17,16},{19,... | collective-permute-start | bytes 101384 | tf_op jit(solution)/shard_map/ppermute | solution.py:20
  48.3 3.2 %collective-permute-start.8 = (f32[1152,256]{1,0:T(8,128)}, f32[1152,256]{1,0:T(8,128)}, u32[]{:S(2)}, u32[]{:S(2)}) collective-permute-start(f32[1152,256]{1,0:T(8,128)} %constant_dynamic-slice_fusion.3), channel_id=1, source_target_pairs={{0,1},{1,0},{2,3},{3,2},{4,5},{5,4},{6,7},{7,6},{8,9},{9,8},{10,11... | collective-permute-start | bytes 3538952 | tf_op jit(solution)/shard_map/ppermute | solution.py:199
  55.1 16.2 %collective-permute-start.9 = (f32[576,256]{1,0:T(8,128)S(1)}, f32[576,256]{1,0:T(8,128)S(1)}, u32[]{:S(2)}, u32[]{:S(2)}) collective-permute-start(f32[576,256]{1,0:T(8,128)S(1)} %constant_dynamic-slice_fusion.2), channel_id=1, source_target_pairs={{0,2},{2,0},{4,6},{6,4},{8,10},{10,8},{12,14},{14,12},{1,3},{3,1},... | collective-permute-start | bytes 1769480 | tf_op jit(solution)/shard_map/ppermute | solution.py:199
  72.5 9.3 %collective-permute-start.10 = (f32[288,256]{1,0:T(8,128)S(1)}, f32[288,256]{1,0:T(8,128)S(1)}, u32[]{:S(2)}, u32[]{:S(2)}) collective-permute-start(f32[288,256]{1,0:T(8,128)S(1)} %constant_dynamic-slice_fusion.1), channel_id=1, source_target_pairs={{0,4},{2,6},{4,0},{6,2},{8,12},{10,14},{12,8},{14,10},{1,5},{3,7},... | collective-permute-start | bytes 884744 | tf_op jit(solution)/shard_map/ppermute | solution.py:199
  81.8 8.6 %collective-permute-start.11 = (f32[144,256]{1,0:T(8,128)S(1)}, f32[144,256]{1,0:T(8,128)S(1)}, u32[]{:S(2)}, u32[]{:S(2)}) collective-permute-start(f32[144,256]{1,0:T(8,128)S(1)} %constant_dynamic-slice_fusion), channel_id=1, source_target_pairs={{0,8},{2,10},{4,12},{6,14},{8,0},{10,2},{12,4},{14,6},{1,9},{3,11}... | collective-permute-start | bytes 442376 | tf_op jit(solution)/shard_map/ppermute | solution.py:199
  90.4 6.1 %collective-permute-start.12 = (bf16[144,256]{1,0:T(8,128)(2,1)S(1)}, bf16[144,256]{1,0:T(8,128)(2,1)S(1)}, u32[]{:S(2)}, u32[]{:S(2)}) collective-permute-start(bf16[144,256]{1,0:T(8,128)(2,1)S(1)} %get-tuple-element.80), channel_id=1, source_target_pairs={{0,8},{2,10},{4,12},{6,14},{8,0},{10,2},{12,4},{14,6},{1,9},{3,11}... | collective-permute-start | bytes 221192 | tf_op jit(solution)/shard_map/ppermute | solution.py:206
  90.9 10.4 %collective-permute-start.4 = (f32[3,32,256]{2,1,0:T(8,128)S(1)}, f32[3,32,256]{2,1,0:T(8,128)S(1)}, u32[]{:S(2)}, u32[]{:S(2)}) collective-permute-start(f32[3,32,256]{2,1,0:T(8,128)S(1)} %get-tuple-element.97), channel_id=1, source_target_pairs={{0,2},{2,4},{4,6},{6,8},{8,10},{10,12},{12,14},{1,3},{3,5},{5,7},{... | collective-permute-start | bytes 294920 | tf_op jit(solution)/shard_map/ppermute | solution.py:17
  93.4 8.9 %collective-permute-start.5 = (f32[3,32,256]{2,1,0:T(8,128)S(1)}, f32[3,32,256]{2,1,0:T(8,128)S(1)}, u32[]{:S(2)}, u32[]{:S(2)}) collective-permute-start(f32[3,32,256]{2,1,0:T(8,128)S(1)} %get-tuple-element.98), channel_id=1, source_target_pairs={{2,0},{4,2},{6,4},{8,6},{10,8},{12,10},{14,12},{3,1},{5,3},{7,5},{... | collective-permute-start | bytes 294920 | tf_op jit(solution)/shard_map/ppermute | solution.py:20
  96.5 10.4 %collective-permute-start.13 = (bf16[288,256]{1,0:T(8,128)(2,1)S(1)}, bf16[288,256]{1,0:T(8,128)(2,1)S(1)}, u32[]{:S(2)}, u32[]{:S(2)}) collective-permute-start(bf16[288,256]{1,0:T(8,128)(2,1)S(1)} %constant_dynamic-update-slice_fusion.13), channel_id=1, source_target_pairs={{0,4},{2,6},{4,0},{6,2},{8,12},{10,14},{12,8},{14,10},{1,5},{3,7},... | collective-permute-start | bytes 442376 | tf_op jit(solution)/shard_map/ppermute | solution.py:206
  102.3 8.1 %collective-permute-start.6 = (f32[22,3,256]{2,1,0:T(4,128)S(1)}, f32[22,3,256]{2,1,0:T(4,128)S(1)}, u32[]{:S(2)}, u32[]{:S(2)}) collective-permute-start(f32[22,3,256]{2,1,0:T(4,128)S(1)} %get-tuple-element.95), channel_id=1, source_target_pairs={{1,0},{3,2},{5,4},{7,6},{9,8},{11,10},{13,12},{15,14},{17,16},{19,... | collective-permute-start | bytes 202760 | tf_op jit(solution)/shard_map/ppermute | solution.py:20
  103.6 6.8 %collective-permute-start.7 = (f32[22,3,256]{2,1,0:T(4,128)S(1)}, f32[22,3,256]{2,1,0:T(4,128)S(1)}, u32[]{:S(2)}, u32[]{:S(2)}) collective-permute-start(f32[22,3,256]{2,1,0:T(4,128)S(1)} %get-tuple-element.96), channel_id=1, source_target_pairs={{0,1},{2,3},{4,5},{6,7},{8,9},{10,11},{12,13},{14,15},{16,17},{18,... | collective-permute-start | bytes 202760 | tf_op jit(solution)/shard_map/ppermute | solution.py:17
  107.3 9.7 %collective-permute-start.14 = (bf16[576,256]{1,0:T(8,128)(2,1)S(1)}, bf16[576,256]{1,0:T(8,128)(2,1)S(1)}, u32[]{:S(2)}, u32[]{:S(2)}) collective-permute-start(bf16[576,256]{1,0:T(8,128)(2,1)S(1)} %constant_dynamic-update-slice_fusion.11), channel_id=1, source_target_pairs={{0,2},{2,0},{4,6},{6,4},{8,10},{10,8},{12,14},{14,12},{1,3},{3,1},... | collective-permute-start | bytes 884744 | tf_op jit(solution)/shard_map/ppermute | solution.py:206
  117.0 5.2 %collective-permute-start.15 = (bf16[1152,256]{1,0:T(8,128)(2,1)S(1)}, bf16[1152,256]{1,0:T(8,128)(2,1)S(1)}, u32[]{:S(2)}, u32[]{:S(2)}) collective-permute-start(bf16[1152,256]{1,0:T(8,128)(2,1)S(1)} %constant_dynamic-update-slice_fusion.9), channel_id=1, source_target_pairs={{0,1},{1,0},{2,3},{3,2},{4,5},{5,4},{6,7},{7,6},{8,9},{9,8},{10,11... | collective-permute-start | bytes 1769480 | tf_op jit(solution)/shard_map/ppermute | solution.py:206
  (63 other events, 567.3 us)

commit v3 on v0

--- a/solution.py
+++ b/solution.py
@@ -90,6 +90,68 @@
     return (flat_parts, normed, grad_conv)
 
 
+def halving_stages(sizes):
+    stages = []
+    for axis, count in sizes:
+        bit = 1
+        while bit < count:
+            stages.append((axis, count, bit))
+            bit *= 2
+    return stages
+
+
+def stage_side(axis, bit):
+    return (lax.axis_index(axis) // bit) % 2
+
+
+def stage_pairs(count, bit):
+    return [(i, i ^ bit) for i in range(count)]
+
+
+def halving_reduce_scatter(block, stages):
+    for axis, count, bit in stages:
+        half = block.shape[0] // 2
+        side = stage_side(axis, bit)
+        kept = lax.dynamic_slice_in_dim(block, side * half, half, axis=0)
+        sent = lax.dynamic_slice_in_dim(block, (1 - side) * half, half, axis=0)
+        block = kept + lax.ppermute(sent, axis, stage_pairs(count, bit))
+    return block
+
+
+def doubling_all_gather(block, stages):
+    for axis, count, bit in reversed(stages):
+        side = stage_side(axis, bit)
+        other = lax.ppermute(block, axis, stage_pairs(count, bit))
+        full = jnp.zeros((2 * block.shape[0],) + block.shape[1:], block.dtype)
+        full = lax.dynamic_update_slice_in_dim(full, block, side * block.shape[0], axis=0)
+        block = lax.dynamic_update_slice_in_dim(full, other, (1 - side) * block.shape[0], axis=0)
+    return block
+
+
+def group_all_reduce(block, sizes, scale):
+    stages = halving_stages(sizes)
+    block = halving_reduce_scatter(block, stages) * scale
+    return doubling_all_gather(block.astype(jnp.bfloat16), stages).astype(jnp.float32)
+
+
+def pack_rows(pieces, channels, unit):
+    flat = [piece.reshape(-1, channels) for piece in pieces]
+    rows = sum(piece.shape[0] for piece in flat)
+    if rows % unit:
+        flat.append(jnp.zeros(((-rows) % unit, channels), jnp.float32))
+    return jnp.concatenate(flat, axis=0)
+
+
+def unpack_rows(packed, pieces, channels):
+    parts = []
+    at = 0
+    for piece in pieces:
+        count = piece.size // channels
+        parts.append(packed[at : at + count].reshape(piece.shape))
+        at += count
+    return parts
+
+
 def per_device(
     feature_map,
     cotangent,
@@ -122,7 +184,7 @@
     trimmed = [element for element in flat_parts]
     flat_in, hidden, branch, upstream, grad_branch, grad_branch_b, grad_pre, grad_scaled = trimmed
     grad_w_in = lax.dot_general(
-        flat_in, grad_pre, contract_first, preferred_element_type=jnp.float32
+        grad_pre, flat_in, contract_first, preferred_element_type=jnp.float32
     )
     grad_b_in = jnp.sum(grad_pre.astype(jnp.float32), axis=0)
     grad_w_out = lax.dot_general(
@@ -143,7 +205,7 @@
                 axis=(0, 1),
             )
         )
-    grad_kernel = jnp.stack(tap_sums)
+    grad_kernel = lax.optimization_barrier(jnp.stack(tap_sums))
     grad_kbias = jnp.sum(grad_conv_full, axis=(0, 1))
     running_input = cotangent.astype(jnp.float32)
     for tap_index in range(KS * KS):
@@ -153,32 +215,33 @@
             + grad_pad[6 - row_off : 6 - row_off + tile_rows, 6 - col_off : 6 - col_off + tile_cols]
             * kernel[tap_index]
         )
-    totals = lax.psum(
-        (
-            grad_kernel,
-            grad_kbias,
-            grad_gain,
-            grad_shift,
-            grad_w_in,
-            grad_b_in,
-            grad_w_out,
-            grad_b_out,
-            grad_scale,
-        ),
-        ("row", "col"),
-    )
     divisor = 4.0 * lax.axis_size("row")
+    sizes = (("col", lax.axis_size("col")), ("row", lax.axis_size("row")))
+    unit = 8 * lax.axis_size("col") * lax.axis_size("row")
+    early = [grad_b_in, grad_b_out, grad_scale]
+    early_block = pack_rows(early, channels, 8)
+    packed = pack_rows([grad_w_out, early_block], channels, unit)
+    packed = group_all_reduce(packed, sizes, 1.0 / divisor)
+    w_out, early_block = unpack_rows(packed, [grad_w_out, early_block], channels)
+    g_b_in, g_b_out, g_scale = unpack_rows(early_block, early, channels)
+    late = [grad_kernel, grad_kbias, grad_gain, grad_shift]
+    late_block = pack_rows(late, channels, 8)
+    packed = pack_rows([grad_w_in, late_block], channels, unit)
+    packed = group_all_reduce(packed, sizes, 1.0 / divisor)
+    w_in, late_block = unpack_rows(packed, [grad_w_in, late_block], channels)
+    w_in = w_in.T
+    g_kernel, g_kbias, g_gain, g_shift = unpack_rows(late_block, late, channels)
     return (
         running_input.astype(jnp.bfloat16),
-        totals[0] / divisor,
-        totals[1] / divisor,
-        totals[2] / divisor,
-        totals[3] / divisor,
-        totals[4] / divisor,
-        totals[5] / divisor,
-        totals[6] / divisor,
-        totals[7] / divisor,
-        totals[8] / divisor,
+        g_kernel,
+        g_kbias,
+        g_gain,
+        g_shift,
+        w_in,
+        g_b_in,
+        w_out,
+        g_b_out,
+        g_scale,
     )
 
 

time: 223 us -> 119 us (0.53)
  waiting for transfers between devices: 88.3 us -> 21.6 us
  blocking collectives: 63.6 us -> 0 us
  starting transfers between devices: 16 us -> 44.9 us
  between operations: 15.5 us -> 2.66 us
  local copies, waits for them, and re-layouts: 5.63 us -> 18.2 us
    psum x1 -> x0, waiting for transfers between devices: 83.2 us -> none  [per_device(): lax.psum((grad_kernel, grad_kbias, grad_gain, grad_shift, grad_w_in, grad...]
    psum x1 -> x0, blocking collectives: 63.6 us -> none  [per_device(): lax.psum((grad_kernel, grad_kbias, grad_gain, grad_shift, grad_w_in, grad...]
    ppermute x0 -> x16, starting transfers between devices: none -> 25.2 us  [the longest x8 13.9 us: halving_reduce_scatter(): block = kept + lax.ppermute(sent, axis, stage_pairs(count, bit))]
    ppermute x0 -> x16, waiting for transfers between devices: none -> 19.4 us  [the longest x8 14.2 us: halving_reduce_scatter(): block = kept + lax.ppermute(sent, axis, stage_pairs(count, bit))]
    div x7 -> x0, other arithmetic: 6.37 us -> none  [the longest x1 2.35 us: per_device(): totals[6] / divisor]
    concatenate x0 -> x2, local copies, waits for them, and re-layouts: none -> 4.84 us  [pack_rows(): return jnp.concatenate(flat, axis=0)]
    ppermute x4, starting transfers between devices: 10.8 us -> 14.5 us  [with_halo(): lax.ppermute(lax.slice_in_dim(block, block.shape[dim] - width, None, axis...]
    slice x0 -> x4, local copies, waits for them, and re-layouts: none -> 2.82 us  [unpack_rows(): parts.append(packed[at:at + count].reshape(piece.shape))]
  transfers between devices with their start and end apart: 9 -> 24, of which waited for: 5 -> 11; matrix products, arithmetic and copies ran while one was open for 6% -> 19% of each run, Pallas kernels for 0% -> 0%
where the time goes in v3:
time: 119 us; the launch traced here: 118 us
  starting transfers between devices  44.9 us (38%)
  other arithmetic  22.8 us (19%)
  waiting for transfers between devices  21.6 us (18%)
  local copies, waits for them, and re-layouts  18.2 us (15%)
  matrix products  8.28 us (7%)
  between operations  2.66 us (2%)
    ppermute x4, starting transfers between devices, with_halo(): lax.ppermute(lax.slice_in_dim(block, block.shape[dim] - width, None, axis...  14.5 us
    ppermute x8, waiting for transfers between devices, halving_reduce_scatter(): block = kept + lax.ppermute(sent, axis, stage_pairs(count, bit))  14.2 us
    ppermute x8, starting transfers between devices, halving_reduce_scatter(): block = kept + lax.ppermute(sent, axis, stage_pairs(count, bit))  13.9 us
    ppermute x8, starting transfers between devices, doubling_all_gather(): other = lax.ppermute(block, axis, stage_pairs(count, bit))  11.3 us
    reduce_sum x1, other arithmetic, forward_back(): centred = conv_out - jnp.mean(conv_out, axis=2, keepdims=True)  6.42 us
    convert_element_type x1, other arithmetic, per_device(): running_input.astype(jnp.bfloat16)  5.72 us
    ppermute x8, waiting for transfers between devices, doubling_all_gather(): other = lax.ppermute(block, axis, stage_pairs(count, bit))  5.21 us
    ppermute x4, starting transfers between devices, with_halo(): lax.ppermute(lax.slice_in_dim(block, 0, width, axis=dim), axis, backward)  5.16 us
  transfers between devices with their start and end apart: 24, of which 11 were waited for; matrix products, arithmetic and copies ran while one was open for 19% of the time, Pallas kernels for 0%

profile of v3, /device:TPU:0, one launch (start us, length us, event | category | flops | bytes accessed | tf_op | source)
XLA Modules:
  0.0 118.4 jit_solution(16120237000058604481)
XLA Ops:
  1.6 4.9 %collective-permute-start = (bf16[3,32,256]{2,1,0:T(8,128)(2,1)S(1)}, bf16[3,32,256]{2,1,0:T(8,128)(2,1)S(1)}, u32[]{:S(2)}, u32[]{:S(2)}) collective-permute-start(bf16[3,32,256]{2,1,0:T(8,128)(2,1)S(1)} %get-tuple-element.105), channel_id=1, source_target_pairs={{0,2},{2,4},{4,6},{6,8},{8,10},{10,12},{12,14},{1,3},{3,5},{5,7},{... | collective-permute-start | bytes 147464 | tf_op jit(solution)/shard_map/ppermute | solution.py:14
  6.5 1.3 %collective-permute-start.1 = (bf16[3,32,256]{2,1,0:T(8,128)(2,1)S(1)}, bf16[3,32,256]{2,1,0:T(8,128)(2,1)S(1)}, u32[]{:S(2)}, u32[]{:S(2)}) collective-permute-start(bf16[3,32,256]{2,1,0:T(8,128)(2,1)S(1)} %get-tuple-element.104), channel_id=1, source_target_pairs={{2,0},{4,2},{6,4},{8,6},{10,8},{12,10},{14,12},{3,1},{5,3},{7,5},{... | collective-permute-start | bytes 147464 | tf_op jit(solution)/shard_map/ppermute | solution.py:17
  11.3 1.6 %fusion.218 = (f32[1,256]{1,0:T(1,128)S(1)}, f32[1,256]{1,0:T(1,128)}, f32[1,256]{1,0:T(1,128)}, f32[1,256]{1,0:T(1,128)}, f32[1,256]{1,0:T(1,128)}, /*index=5*/...) fusion(f32[49,256]{1,0:T(8,128)} %param.13), kind=kLoop, calls=%fused_computation.513 | loop fusion | bytes 22528 | tf_op jit(solution)/shard_map/slice | solution.py:35
  14.0 1.5 %collective-permute-start.2 = (bf16[22,3,256]{2,1,0:T(4,128)(2,1)S(1)}, bf16[22,3,256]{2,1,0:T(4,128)(2,1)S(1)}, u32[]{:S(2)}, u32[]{:S(2)}) collective-permute-start(bf16[22,3,256]{2,1,0:T(4,128)(2,1)S(1)} %get-tuple-element.99), channel_id=1, source_target_pairs={{0,1},{2,3},{4,5},{6,7},{8,9},{10,11},{12,13},{14,15},{16,17},{18,... | collective-permute-start | bytes 101384 | tf_op jit(solution)/shard_map/ppermute | solution.py:14
  15.5 1.3 %collective-permute-start.3 = (bf16[22,3,256]{2,1,0:T(4,128)(2,1)S(1)}, bf16[22,3,256]{2,1,0:T(4,128)(2,1)S(1)}, u32[]{:S(2)}, u32[]{:S(2)}) collective-permute-start(bf16[22,3,256]{2,1,0:T(4,128)(2,1)S(1)} %get-tuple-element.100), channel_id=1, source_target_pairs={{1,0},{3,2},{5,4},{7,6},{9,8},{11,10},{13,12},{15,14},{17,16},{19,... | collective-permute-start | bytes 101384 | tf_op jit(solution)/shard_map/ppermute | solution.py:17
  18.6 6.4 %fusion.209 = (f32[16,32]{1,0:T(8,128)S(1)}, f32[16,32,256]{2,1,0:T(8,128)S(1)}) fusion(f32[256]{0:T(256)S(1)} %copy-done.99, f32[256]{0:T(256)} %bitcast.49, bf16[22,3,256]{2,1,0:T(4,128)(2,1)S(1)} %collective-permute-done.3, bf16[22,32,256]{2,1,0:T(8,128)(2,1)S(1)} %get-tuple-element.158, f32[256]{0:T(256)} %bitcast.48, f32[256]{0:T(256)S(1)} %bitcast.144, ...), kind=kLoop, calls=%fused_computation.505 | loop fusion | flops 35913216 | bytes 2840576 | tf_op jit(solution)/shard_map/reduce_sum | solution.py:56
  26.0 1.6 %multiply_convert_fusion = (bf16[512,1024]{1,0:T(8,128)(2,1)}, f32[512,1024]{1,0:T(8,128)S(1)}) fusion(f32[1024]{0:T(1024)S(1)} %copy-done.85, bf16[512,256]{1,0:T(8,128)(2,1)S(1)} %bitcast.140, bf16[256,1024]{1,0:T(8,128)(2,1)S(1)} %copy-done), kind=kOutput, calls=%fused_computation.48 | convolution fusion | flops 271581184 | bytes 3936256 | tf_op jit(solution)/shard_map/dot_general | solution.py:60
  27.6 1.3 %convert_reduce_fusion = (f32[1024]{0:T(1024)S(1)}, bf16[512,1024]{1,0:T(8,128)(2,1)S(1)}) fusion(f32[512,1024]{1,0:T(8,128)S(1)} %get-tuple-element.161, f32[1024]{0:T(1024)S(1)} %copy-done.85, bf16[512,256]{1,0:T(8,128)(2,1)S(1)} %fusion.165, bf16[1024,256]{1,0:T(8,128)(2,1)S(1)} %copy-done.101), kind=kOutput, calls=%fused_computation.47 | convolution fusion | flops 275250176 | bytes 3940352 | tf_op jit(solution)/shard_map/dot_general | solution.py:67
  28.9 1.5 %fusion.219 = f32[1024,256]{1,0:T(8,128)} fusion(bf16[512,1024]{1,0:T(8,128)(2,1)S(1)} %get-tuple-element.163, bf16[512,256]{1,0:T(8,128)(2,1)S(1)} %bitcast.141), kind=kOutput, calls=%fused_computation.514 | convolution fusion | flops 268435456 | bytes 2359296 | tf_op jit(solution)/shard_map/dot_general | solution.py:186
  31.7 1.7 %fusion.158 = (f32[256]{0:T(256)S(1)}, f32[256]{0:T(256)S(1)}, f32[256]{0:T(256)S(1)}, f32[256]{0:T(256)S(1)}, f32[256]{0:T(256)S(1)}, /*index=5*/f32[256]{0:T(2...) fusion(bf16[22,3,256]{2,1,0:T(4,128)(2,1)S(1)} %collective-permute-done.3, ...), kind=kLoop, calls=%fused_computation.314 | loop fusion | flops 7730944 | bytes 1983488 | tf_op jit(solution)/shard_map/reduce_sum | solution.py:202
  35.0 2.4 %fusion.220 = f32[1024,256]{1,0:T(8,128)} fusion(bf16[512,1024]{1,0:T(8,128)(2,1)S(1)} %copy-done.1, bf16[512,256]{1,0:T(8,128)(2,1)} %copy-done.6), kind=kOutput, calls=%fused_computation.515 | convolution fusion | flops 268435456 | bytes 2359296 | tf_op jit(solution)/shard_map/dot_general | solution.py:190
  37.9 2.1 %concatenate.137 = f32[1152,256]{1,0:T(8,128)S(1)} concatenate(f32[1024,256]{1,0:T(8,128)} %fusion.220, f32[4,256]{1,0:T(4,128)S(1)} %reshape.162, f32[1,256]{1,0:T(1,128)S(1)} %bitcast.223, f32[1,256]{1,0:T(1,128)S(1)} %bitcast.274, f32[2,256]{1,0:T(2,128)S(1)} %broadcast_in_dim.10, f32[120,256]{1,0:T(8,128)S(1)} %broadcast_in_dim.11), dimensions={0} | concatenate | bytes 2359296 | tf_op jit(solution)/shard_map/concatenate | solution.py:142
  41.2 5.0 %collective-permute-start.4 = (f32[3,32,256]{2,1,0:T(8,128)}, f32[3,32,256]{2,1,0:T(8,128)}, u32[]{:S(2)}, u32[]{:S(2)}) collective-permute-start(f32[3,32,256]{2,1,0:T(8,128)} %get-tuple-element.97), channel_id=1, source_target_pairs={{0,2},{2,4},{4,6},{6,8},{8,10},{10,12},{12,14},{1,3},{3,5},{5,7},{... | collective-permute-start | bytes 294920 | tf_op jit(solution)/shard_map/ppermute | solution.py:14
  49.9 2.8 %concatenate.136 = f32[1152,256]{1,0:T(8,128)S(1)} concatenate(f32[1024,256]{1,0:T(8,128)} %fusion.219, f32[49,256]{1,0:T(8,128)S(1)} %stack.199, f32[1,256]{1,0:T(1,128)} %bitcast.222, f32[1,256]{1,0:T(1,128)} %bitcast.221, f32[1,256]{1,0:T(1,128)S(1)} %bitcast.220, f32[4,256]{1,0:T(4,128)S(1)} %broadcast_in_dim.8, f32[72,256]{1,0:T(8,128)S(1)} %broadcast_in_dim.9), dimensions={0} | concatenate | bytes 2359296 | tf_op jit(solution)/shard_map/concatenate | solution.py:142
  54.5 1.3 %collective-permute-start.6 = (f32[22,3,256]{2,1,0:T(4,128)S(1)}, f32[22,3,256]{2,1,0:T(4,128)S(1)}, u32[]{:S(2)}, u32[]{:S(2)}) collective-permute-start(f32[22,3,256]{2,1,0:T(4,128)S(1)} %get-tuple-element.90), channel_id=1, source_target_pairs={{1,0},{3,2},{5,4},{7,6},{9,8},{11,10},{13,12},{15,14},{17,16},{19,... | collective-permute-start | bytes 202760 | tf_op jit(solution)/shard_map/ppermute | solution.py:17
  55.8 3.2 %collective-permute-start.7 = (f32[22,3,256]{2,1,0:T(4,128)S(1)}, f32[22,3,256]{2,1,0:T(4,128)S(1)}, u32[]{:S(2)}, u32[]{:S(2)}) collective-permute-start(f32[22,3,256]{2,1,0:T(4,128)S(1)} %get-tuple-element.91), channel_id=1, source_target_pairs={{0,1},{2,3},{4,5},{6,7},{8,9},{10,11},{12,13},{14,15},{16,17},{18,... | collective-permute-start | bytes 202760 | tf_op jit(solution)/shard_map/ppermute | solution.py:14
  61.3 5.7 %fusion.167 = bf16[16,32,256]{2,1,0:T(8,128)(2,1)} fusion(f32[22,35,256]{2,1,0:T(8,128)S(1)} %get-tuple-element.89, f32[16,32,256]{2,1,0:T(8,128)S(1)} %get-tuple-element.83, f32[3,32,256]{2,1,0:T(8,128)} %collective-permute-done.4, f32[22,35,256]{2,1,0:T(8,128)S(1)} %get-tuple-element.88, f32[3,32,256]{2,1,0:T(8,128)} %collective-permute-done.5, ...), kind=kLoop, calls=%fused_computation.375 | loop fusion | flops 13893632 | bytes 23315456 | tf_op jit(solution)/shard_map/convert_element_type | solution.py:235
  68.2 2.7 %collective-permute-start.17 = (f32[288,256]{1,0:T(8,128)S(1)}, f32[288,256]{1,0:T(8,128)S(1)}, u32[]{:S(2)}, u32[]{:S(2)}) collective-permute-start(f32[288,256]{1,0:T(8,128)S(1)} %constant_dynamic-slice_fusion.2), channel_id=1, source_target_pairs={{0,2},{2,0},{4,6},{6,4},{8,10},{10,8},{12,14},{14,12},{1,3},{3,1},... | collective-permute-start | bytes 884744 | tf_op jit(solution)/shard_map/ppermute | solution.py:117
  71.1 7.6 %collective-permute-done.17 = f32[288,256]{1,0:T(8,128)S(1)} collective-permute-done((f32[288,256]{1,0:T(8,128)S(1)}, f32[288,256]{1,0:T(8,128)S(1)}, u32[]{:S(2)}, u32[]{:S(2)}) %collective-permute-start.17) | collective-permute-done | bytes 294944 | tf_op jit(solution)/shard_map/ppermute | solution.py:117
  78.8 2.8 %collective-permute-start.18 = (f32[144,256]{1,0:T(8,128)S(1)}, f32[144,256]{1,0:T(8,128)S(1)}, u32[]{:S(2)}, u32[]{:S(2)}) collective-permute-start(f32[144,256]{1,0:T(8,128)S(1)} %constant_dynamic-slice_fusion.1), channel_id=1, source_target_pairs={{0,4},{2,6},{4,0},{6,2},{8,12},{10,14},{12,8},{14,10},{1,5},{3,7},... | collective-permute-start | bytes 442376 | tf_op jit(solution)/shard_map/ppermute | solution.py:117
  81.7 3.1 %collective-permute-done.9 = f32[288,256]{1,0:T(8,128)S(1)} collective-permute-done((f32[288,256]{1,0:T(8,128)S(1)}, f32[288,256]{1,0:T(8,128)S(1)}, u32[]{:S(2)}, u32[]{:S(2)}) %collective-permute-start.9) | collective-permute-done | bytes 294944 | tf_op jit(solution)/shard_map/ppermute | solution.py:117
  84.8 2.5 %collective-permute-start.10 = (f32[144,256]{1,0:T(8,128)S(1)}, f32[144,256]{1,0:T(8,128)S(1)}, u32[]{:S(2)}, u32[]{:S(2)}) collective-permute-start(f32[144,256]{1,0:T(8,128)S(1)} %constant_dynamic-slice_fusion.5), channel_id=1, source_target_pairs={{0,4},{2,6},{4,0},{6,2},{8,12},{10,14},{12,8},{14,10},{1,5},{3,7},... | collective-permute-start | bytes 442376 | tf_op jit(solution)/shard_map/ppermute | solution.py:117
  87.4 2.6 %collective-permute-start.19 = (f32[72,256]{1,0:T(8,128)S(1)}, f32[72,256]{1,0:T(8,128)S(1)}, u32[]{:S(2)}, u32[]{:S(2)}) collective-permute-start(f32[72,256]{1,0:T(8,128)S(1)} %constant_dynamic-slice_fusion), channel_id=1, source_target_pairs={{0,8},{2,10},{4,12},{6,14},{8,0},{10,2},{12,4},{14,6},{1,9},{3,11}... | collective-permute-start | bytes 221192 | tf_op jit(solution)/shard_map/ppermute | solution.py:117
  90.1 1.6 %collective-permute-done.10 = f32[144,256]{1,0:T(8,128)S(1)} collective-permute-done((f32[144,256]{1,0:T(8,128)S(1)}, f32[144,256]{1,0:T(8,128)S(1)}, u32[]{:S(2)}, u32[]{:S(2)}) %collective-permute-start.10) | collective-permute-done | bytes 147488 | tf_op jit(solution)/shard_map/ppermute | solution.py:117
  91.7 2.8 %collective-permute-start.11 = (f32[72,256]{1,0:T(8,128)S(1)}, f32[72,256]{1,0:T(8,128)S(1)}, u32[]{:S(2)}, u32[]{:S(2)}) collective-permute-start(f32[72,256]{1,0:T(8,128)S(1)} %constant_dynamic-slice_fusion.4), channel_id=1, source_target_pairs={{0,8},{2,10},{4,12},{6,14},{8,0},{10,2},{12,4},{14,6},{1,9},{3,11}... | collective-permute-start | bytes 221192 | tf_op jit(solution)/shard_map/ppermute | solution.py:117
  95.4 1.8 %collective-permute-done.11 = f32[72,256]{1,0:T(8,128)S(1)} collective-permute-done((f32[72,256]{1,0:T(8,128)S(1)}, f32[72,256]{1,0:T(8,128)S(1)}, u32[]{:S(2)}, u32[]{:S(2)}) %collective-permute-start.11) | collective-permute-done | bytes 73760 | tf_op jit(solution)/shard_map/ppermute | solution.py:117
  97.2 2.6 %collective-permute-start.12 = (bf16[72,256]{1,0:T(8,128)(2,1)S(1)}, bf16[72,256]{1,0:T(8,128)(2,1)S(1)}, u32[]{:S(2)}, u32[]{:S(2)}) collective-permute-start(bf16[72,256]{1,0:T(8,128)(2,1)S(1)} %get-tuple-element.82), channel_id=1, source_target_pairs={{0,8},{2,10},{4,12},{6,14},{8,0},{10,2},{12,4},{14,6},{1,9},{3,11}... | collective-permute-start | bytes 110600 | tf_op jit(solution)/shard_map/ppermute | solution.py:124
  100.0 3.2 %collective-permute-start.21 = (bf16[144,256]{1,0:T(8,128)(2,1)S(1)}, bf16[144,256]{1,0:T(8,128)(2,1)S(1)}, u32[]{:S(2)}, u32[]{:S(2)}) collective-permute-start(bf16[144,256]{1,0:T(8,128)(2,1)S(1)} %constant_dynamic-update-slice_fusion.13), channel_id=1, source_target_pairs={{0,4},{2,6},{4,0},{6,2},{8,12},{10,14},{12,8},{14,10},{1,5},{3,7},... | collective-permute-start | bytes 221192 | tf_op jit(solution)/shard_map/ppermute | solution.py:124
  103.3 2.2 %collective-permute-start.13 = (bf16[144,256]{1,0:T(8,128)(2,1)S(1)}, bf16[144,256]{1,0:T(8,128)(2,1)S(1)}, u32[]{:S(2)}, u32[]{:S(2)}) collective-permute-start(bf16[144,256]{1,0:T(8,128)(2,1)S(1)} %constant_dynamic-update-slice_fusion.21), channel_id=1, source_target_pairs={{0,4},{2,6},{4,0},{6,2},{8,12},{10,14},{12,8},{14,10},{1,5},{3,7},... | collective-permute-start | bytes 221192 | tf_op jit(solution)/shard_map/ppermute | solution.py:124
  109.0 1.8 %collective-permute-done.22 = bf16[288,256]{1,0:T(8,128)(2,1)S(1)} collective-permute-done((bf16[288,256]{1,0:T(8,128)(2,1)S(1)}, bf16[288,256]{1,0:T(8,128)(2,1)S(1)}, u32[]{:S(2)}, u32[]{:S(2)}) %collective-permute-start.22) | collective-permute-done | bytes 147488 | tf_op jit(solution)/shard_map/ppermute | solution.py:124
  110.9 2.2 %collective-permute-done.14 = bf16[288,256]{1,0:T(8,128)(2,1)S(1)} collective-permute-done((bf16[288,256]{1,0:T(8,128)(2,1)S(1)}, bf16[288,256]{1,0:T(8,128)(2,1)S(1)}, u32[]{:S(2)}, u32[]{:S(2)}) %collective-permute-start.14) | collective-permute-done | bytes 147488 | tf_op jit(solution)/shard_map/ppermute | solution.py:124
  117.1 1.3 %copy.21 = f32[256,1024]{1,0:T(8,128)} copy(f32[256,1024]{0,1:T(8,128)S(1)} %slice_bitcast_fusion) | data formatting | bytes 2097152
  (315 shorter events, 29.4 us)
Async XLA Ops:
  0.6 25.3 %copy-start = (bf16[256,1024]{1,0:T(8,128)(2,1)S(1)}, bf16[256,1024]{1,0:T(8,128)(2,1)}, u32[]{:S(2)}) copy-start(bf16[256,1024]{1,0:T(8,128)(2,1)} %param.17) | copy-start | bytes 1572868
  0.7 17.9 %copy-start.2 = (bf16[16,32,256]{2,1,0:T(8,128)(2,1)S(1)}, bf16[16,32,256]{2,1,0:T(8,128)(2,1)}, u32[]{:S(2)}) copy-start(bf16[16,32,256]{2,1,0:T(8,128)(2,1)} %param.11) | copy-start | bytes 786436
  0.7 17.9 %copy-start.99 = (f32[256]{0:T(256)S(1)}, f32[256]{0:T(256)}, u32[]{:S(2)}) copy-start(f32[256]{0:T(256)} %param.14) | copy-start | bytes 3076
  1.6 11.2 %collective-permute-start = (bf16[3,32,256]{2,1,0:T(8,128)(2,1)S(1)}, bf16[3,32,256]{2,1,0:T(8,128)(2,1)S(1)}, u32[]{:S(2)}, u32[]{:S(2)}) collective-permute-start(bf16[3,32,256]{2,1,0:T(8,128)(2,1)S(1)} %get-tuple-element.105), channel_id=1, source_target_pairs={{0,2},{2,4},{4,6},{6,8},{8,10},{10,12},{12,14},{1,3},{3,5},{5,7},{... | collective-permute-start | bytes 147464 | tf_op jit(solution)/shard_map/ppermute | solution.py:14
  6.5 7.4 %collective-permute-start.1 = (bf16[3,32,256]{2,1,0:T(8,128)(2,1)S(1)}, bf16[3,32,256]{2,1,0:T(8,128)(2,1)S(1)}, u32[]{:S(2)}, u32[]{:S(2)}) collective-permute-start(bf16[3,32,256]{2,1,0:T(8,128)(2,1)S(1)} %get-tuple-element.104), channel_id=1, source_target_pairs={{2,0},{4,2},{6,4},{8,6},{10,8},{12,10},{14,12},{3,1},{5,3},{7,5},{... | collective-permute-start | bytes 147464 | tf_op jit(solution)/shard_map/ppermute | solution.py:17
  8.9 16.2 %copy-start.10 = (f32[1,256]{1,0:T(1,128)}, f32[1,256]{1,0:T(1,128)S(1)}, u32[]{:S(2)}) copy-start(f32[1,256]{1,0:T(1,128)S(1)} %get-tuple-element.108) | copy-start | bytes 3076
  8.9 16.2 %copy-start.12 = (f32[1,256]{1,0:T(1,128)}, f32[1,256]{1,0:T(1,128)S(1)}, u32[]{:S(2)}) copy-start(f32[1,256]{1,0:T(1,128)S(1)} %get-tuple-element.109) | copy-start | bytes 3076
  8.9 16.2 %copy-start.14 = (f32[1,256]{1,0:T(1,128)}, f32[1,256]{1,0:T(1,128)S(1)}, u32[]{:S(2)}) copy-start(f32[1,256]{1,0:T(1,128)S(1)} %get-tuple-element.110) | copy-start | bytes 3076
  8.9 16.2 %copy-start.16 = (f32[1,256]{1,0:T(1,128)}, f32[1,256]{1,0:T(1,128)S(1)}, u32[]{:S(2)}) copy-start(f32[1,256]{1,0:T(1,128)S(1)} %get-tuple-element.111) | copy-start | bytes 3076
  11.3 16.3 %copy-start.6 = (bf16[512,256]{1,0:T(8,128)(2,1)}, bf16[512,256]{1,0:T(8,128)(2,1)S(1)}, u32[]{:S(2)}) copy-start(bf16[512,256]{1,0:T(8,128)(2,1)S(1)} %fusion.165) | copy-start | bytes 786436
  14.0 3.5 %collective-permute-start.2 = (bf16[22,3,256]{2,1,0:T(4,128)(2,1)S(1)}, bf16[22,3,256]{2,1,0:T(4,128)(2,1)S(1)}, u32[]{:S(2)}, u32[]{:S(2)}) collective-permute-start(bf16[22,3,256]{2,1,0:T(4,128)(2,1)S(1)} %get-tuple-element.99), channel_id=1, source_target_pairs={{0,1},{2,3},{4,5},{6,7},{8,9},{10,11},{12,13},{14,15},{16,17},{18,... | collective-permute-start | bytes 101384 | tf_op jit(solution)/shard_map/ppermute | solution.py:14
  15.5 3.1 %collective-permute-start.3 = (bf16[22,3,256]{2,1,0:T(4,128)(2,1)S(1)}, bf16[22,3,256]{2,1,0:T(4,128)(2,1)S(1)}, u32[]{:S(2)}, u32[]{:S(2)}) collective-permute-start(bf16[22,3,256]{2,1,0:T(4,128)(2,1)S(1)} %get-tuple-element.100), channel_id=1, source_target_pairs={{1,0},{3,2},{5,4},{7,6},{9,8},{11,10},{13,12},{15,14},{17,16},{19,... | collective-permute-start | bytes 101384 | tf_op jit(solution)/shard_map/ppermute | solution.py:17
  41.0 26.0 %collective-permute-start.16 = (f32[576,256]{1,0:T(8,128)}, f32[576,256]{1,0:T(8,128)}, u32[]{:S(2)}, u32[]{:S(2)}) collective-permute-start(f32[576,256]{1,0:T(8,128)} %constant_dynamic-slice_fusion.3), channel_id=1, source_target_pairs={{0,1},{1,0},{2,3},{3,2},{4,5},{5,4},{6,7},{7,6},{8,9},{9,8},{10,11... | collective-permute-start | bytes 1769480 | tf_op jit(solution)/shard_map/ppermute | solution.py:117
  41.2 11.5 %collective-permute-start.4 = (f32[3,32,256]{2,1,0:T(8,128)}, f32[3,32,256]{2,1,0:T(8,128)}, u32[]{:S(2)}, u32[]{:S(2)}) collective-permute-start(f32[3,32,256]{2,1,0:T(8,128)} %get-tuple-element.97), channel_id=1, source_target_pairs={{0,2},{2,4},{4,6},{6,8},{8,10},{10,12},{12,14},{1,3},{3,5},{5,7},{... | collective-permute-start | bytes 294920 | tf_op jit(solution)/shard_map/ppermute | solution.py:14
  46.2 7.1 %collective-permute-start.5 = (f32[3,32,256]{2,1,0:T(8,128)}, f32[3,32,256]{2,1,0:T(8,128)}, u32[]{:S(2)}, u32[]{:S(2)}) collective-permute-start(f32[3,32,256]{2,1,0:T(8,128)} %get-tuple-element.98), channel_id=1, source_target_pairs={{2,0},{4,2},{6,4},{8,6},{10,8},{12,10},{14,12},{3,1},{5,3},{7,5},{... | collective-permute-start | bytes 294920 | tf_op jit(solution)/shard_map/ppermute | solution.py:17
  54.5 4.7 %collective-permute-start.6 = (f32[22,3,256]{2,1,0:T(4,128)S(1)}, f32[22,3,256]{2,1,0:T(4,128)S(1)}, u32[]{:S(2)}, u32[]{:S(2)}) collective-permute-start(f32[22,3,256]{2,1,0:T(4,128)S(1)} %get-tuple-element.90), channel_id=1, source_target_pairs={{1,0},{3,2},{5,4},{7,6},{9,8},{11,10},{13,12},{15,14},{17,16},{19,... | collective-permute-start | bytes 202760 | tf_op jit(solution)/shard_map/ppermute | solution.py:17
  55.8 4.0 %collective-permute-start.7 = (f32[22,3,256]{2,1,0:T(4,128)S(1)}, f32[22,3,256]{2,1,0:T(4,128)S(1)}, u32[]{:S(2)}, u32[]{:S(2)}) collective-permute-start(f32[22,3,256]{2,1,0:T(4,128)S(1)} %get-tuple-element.91), channel_id=1, source_target_pairs={{0,1},{2,3},{4,5},{6,7},{8,9},{10,11},{12,13},{14,15},{16,17},{18,... | collective-permute-start | bytes 202760 | tf_op jit(solution)/shard_map/ppermute | solution.py:14
  59.1 11.8 %collective-permute-start.8 = (f32[576,256]{1,0:T(8,128)S(1)}, f32[576,256]{1,0:T(8,128)S(1)}, u32[]{:S(2)}, u32[]{:S(2)}) collective-permute-start(f32[576,256]{1,0:T(8,128)S(1)} %constant_dynamic-slice_fusion.7), channel_id=1, source_target_pairs={{0,1},{1,0},{2,3},{3,2},{4,5},{5,4},{6,7},{7,6},{8,9},{9,8},{10,11... | collective-permute-start | bytes 1769480 | tf_op jit(solution)/shard_map/ppermute | solution.py:117
  68.2 10.6 %collective-permute-start.17 = (f32[288,256]{1,0:T(8,128)S(1)}, f32[288,256]{1,0:T(8,128)S(1)}, u32[]{:S(2)}, u32[]{:S(2)}) collective-permute-start(f32[288,256]{1,0:T(8,128)S(1)} %constant_dynamic-slice_fusion.2), channel_id=1, source_target_pairs={{0,2},{2,0},{4,6},{6,4},{8,10},{10,8},{12,14},{14,12},{1,3},{3,1},... | collective-permute-start | bytes 884744 | tf_op jit(solution)/shard_map/ppermute | solution.py:117
  71.0 13.7 %collective-permute-start.9 = (f32[288,256]{1,0:T(8,128)S(1)}, f32[288,256]{1,0:T(8,128)S(1)}, u32[]{:S(2)}, u32[]{:S(2)}) collective-permute-start(f32[288,256]{1,0:T(8,128)S(1)} %constant_dynamic-slice_fusion.6), channel_id=1, source_target_pairs={{0,2},{2,0},{4,6},{6,4},{8,10},{10,8},{12,14},{14,12},{1,3},{3,1},... | collective-permute-start | bytes 884744 | tf_op jit(solution)/shard_map/ppermute | solution.py:117
  78.8 8.5 %collective-permute-start.18 = (f32[144,256]{1,0:T(8,128)S(1)}, f32[144,256]{1,0:T(8,128)S(1)}, u32[]{:S(2)}, u32[]{:S(2)}) collective-permute-start(f32[144,256]{1,0:T(8,128)S(1)} %constant_dynamic-slice_fusion.1), channel_id=1, source_target_pairs={{0,4},{2,6},{4,0},{6,2},{8,12},{10,14},{12,8},{14,10},{1,5},{3,7},... | collective-permute-start | bytes 442376 | tf_op jit(solution)/shard_map/ppermute | solution.py:117
  84.8 6.8 %collective-permute-start.10 = (f32[144,256]{1,0:T(8,128)S(1)}, f32[144,256]{1,0:T(8,128)S(1)}, u32[]{:S(2)}, u32[]{:S(2)}) collective-permute-start(f32[144,256]{1,0:T(8,128)S(1)} %constant_dynamic-slice_fusion.5), channel_id=1, source_target_pairs={{0,4},{2,6},{4,0},{6,2},{8,12},{10,14},{12,8},{14,10},{1,5},{3,7},... | collective-permute-start | bytes 442376 | tf_op jit(solution)/shard_map/ppermute | solution.py:117
  87.4 7.1 %collective-permute-start.19 = (f32[72,256]{1,0:T(8,128)S(1)}, f32[72,256]{1,0:T(8,128)S(1)}, u32[]{:S(2)}, u32[]{:S(2)}) collective-permute-start(f32[72,256]{1,0:T(8,128)S(1)} %constant_dynamic-slice_fusion), channel_id=1, source_target_pairs={{0,8},{2,10},{4,12},{6,14},{8,0},{10,2},{12,4},{14,6},{1,9},{3,11}... | collective-permute-start | bytes 221192 | tf_op jit(solution)/shard_map/ppermute | solution.py:117
  91.7 5.5 %collective-permute-start.11 = (f32[72,256]{1,0:T(8,128)S(1)}, f32[72,256]{1,0:T(8,128)S(1)}, u32[]{:S(2)}, u32[]{:S(2)}) collective-permute-start(f32[72,256]{1,0:T(8,128)S(1)} %constant_dynamic-slice_fusion.4), channel_id=1, source_target_pairs={{0,8},{2,10},{4,12},{6,14},{8,0},{10,2},{12,4},{14,6},{1,9},{3,11}... | collective-permute-start | bytes 221192 | tf_op jit(solution)/shard_map/ppermute | solution.py:117
  94.6 5.5 %collective-permute-start.20 = (bf16[72,256]{1,0:T(8,128)(2,1)S(1)}, bf16[72,256]{1,0:T(8,128)(2,1)S(1)}, u32[]{:S(2)}, u32[]{:S(2)}) collective-permute-start(bf16[72,256]{1,0:T(8,128)(2,1)S(1)} %get-tuple-element.80), channel_id=1, source_target_pairs={{0,8},{2,10},{4,12},{6,14},{8,0},{10,2},{12,4},{14,6},{1,9},{3,11}... | collective-permute-start | bytes 110600 | tf_op jit(solution)/shard_map/ppermute | solution.py:124
  97.2 6.1 %collective-permute-start.12 = (bf16[72,256]{1,0:T(8,128)(2,1)S(1)}, bf16[72,256]{1,0:T(8,128)(2,1)S(1)}, u32[]{:S(2)}, u32[]{:S(2)}) collective-permute-start(bf16[72,256]{1,0:T(8,128)(2,1)S(1)} %get-tuple-element.82), channel_id=1, source_target_pairs={{0,8},{2,10},{4,12},{6,14},{8,0},{10,2},{12,4},{14,6},{1,9},{3,11}... | collective-permute-start | bytes 110600 | tf_op jit(solution)/shard_map/ppermute | solution.py:124
  100.0 5.5 %collective-permute-start.21 = (bf16[144,256]{1,0:T(8,128)(2,1)S(1)}, bf16[144,256]{1,0:T(8,128)(2,1)S(1)}, u32[]{:S(2)}, u32[]{:S(2)}) collective-permute-start(bf16[144,256]{1,0:T(8,128)(2,1)S(1)} %constant_dynamic-update-slice_fusion.13), channel_id=1, source_target_pairs={{0,4},{2,6},{4,0},{6,2},{8,12},{10,14},{12,8},{14,10},{1,5},{3,7},... | collective-permute-start | bytes 221192 | tf_op jit(solution)/shard_map/ppermute | solution.py:124
  103.3 4.5 %collective-permute-start.13 = (bf16[144,256]{1,0:T(8,128)(2,1)S(1)}, bf16[144,256]{1,0:T(8,128)(2,1)S(1)}, u32[]{:S(2)}, u32[]{:S(2)}) collective-permute-start(bf16[144,256]{1,0:T(8,128)(2,1)S(1)} %constant_dynamic-update-slice_fusion.21), channel_id=1, source_target_pairs={{0,4},{2,6},{4,0},{6,2},{8,12},{10,14},{12,8},{14,10},{1,5},{3,7},... | collective-permute-start | bytes 221192 | tf_op jit(solution)/shard_map/ppermute | solution.py:124
  105.6 5.2 %collective-permute-start.22 = (bf16[288,256]{1,0:T(8,128)(2,1)S(1)}, bf16[288,256]{1,0:T(8,128)(2,1)S(1)}, u32[]{:S(2)}, u32[]{:S(2)}) collective-permute-start(bf16[288,256]{1,0:T(8,128)(2,1)S(1)} %constant_dynamic-update-slice_fusion.11), channel_id=1, source_target_pairs={{0,2},{2,0},{4,6},{6,4},{8,10},{10,8},{12,14},{14,12},{1,3},{3,1},... | collective-permute-start | bytes 442376 | tf_op jit(solution)/shard_map/ppermute | solution.py:124
  107.8 5.2 %collective-permute-start.14 = (bf16[288,256]{1,0:T(8,128)(2,1)S(1)}, bf16[288,256]{1,0:T(8,128)(2,1)S(1)}, u32[]{:S(2)}, u32[]{:S(2)}) collective-permute-start(bf16[288,256]{1,0:T(8,128)(2,1)S(1)} %constant_dynamic-update-slice_fusion.19), channel_id=1, source_target_pairs={{0,2},{2,0},{4,6},{6,4},{8,10},{10,8},{12,14},{14,12},{1,3},{3,1},... | collective-permute-start | bytes 442376 | tf_op jit(solution)/shard_map/ppermute | solution.py:124
  110.8 2.5 %collective-permute-start.23 = (bf16[576,256]{1,0:T(8,128)(2,1)S(1)}, bf16[576,256]{1,0:T(8,128)(2,1)S(1)}, u32[]{:S(2)}, u32[]{:S(2)}) collective-permute-start(bf16[576,256]{1,0:T(8,128)(2,1)S(1)} %constant_dynamic-update-slice_fusion.9), channel_id=1, source_target_pairs={{0,1},{1,0},{2,3},{3,2},{4,5},{5,4},{6,7},{7,6},{8,9},{9,8},{10,11... | collective-permute-start | bytes 884744 | tf_op jit(solution)/shard_map/ppermute | solution.py:124
  113.1 2.0 %collective-permute-start.15 = (bf16[576,256]{1,0:T(8,128)(2,1)S(1)}, bf16[576,256]{1,0:T(8,128)(2,1)S(1)}, u32[]{:S(2)}, u32[]{:S(2)}) collective-permute-start(bf16[576,256]{1,0:T(8,128)(2,1)S(1)} %constant_dynamic-update-slice_fusion.17), channel_id=1, source_target_pairs={{0,1},{1,0},{2,3},{3,2},{4,5},{5,4},{6,7},{7,6},{8,9},{9,8},{10,11... | collective-permute-start | bytes 884744 | tf_op jit(solution)/shard_map/ppermute | solution.py:124
  (96 other events, 977.0 us)

commit v4 on v3

--- a/solution.py
+++ b/solution.py
@@ -128,8 +128,10 @@
     return block
 
 
-def group_all_reduce(block, sizes, scale):
+def group_all_reduce(block, sizes, scale, swap=False):
     stages = halving_stages(sizes)
+    if swap and len(stages) > 2:
+        stages[1], stages[2] = stages[2], stages[1]
     block = halving_reduce_scatter(block, stages) * scale
     return doubling_all_gather(block.astype(jnp.bfloat16), stages).astype(jnp.float32)
 
@@ -227,7 +229,7 @@
     late = [grad_kernel, grad_kbias, grad_gain, grad_shift]
     late_block = pack_rows(late, channels, 8)
     packed = pack_rows([grad_w_in, late_block], channels, unit)
-    packed = group_all_reduce(packed, sizes, 1.0 / divisor)
+    packed = group_all_reduce(packed, sizes, 1.0 / divisor, swap=True)
     w_in, late_block = unpack_rows(packed, [grad_w_in, late_block], channels)
     w_in = w_in.T
     g_kernel, g_kbias, g_gain, g_shift = unpack_rows(late_block, late, channels)

time: 119 us -> 116 us (0.975)
  starting transfers between devices: 44.9 us -> 42 us
    ppermute x8, starting transfers between devices: 11.3 us -> 9.85 us  [doubling_all_gather(): other = lax.ppermute(block, axis, stage_pairs(count, bit))]
    ppermute x8, starting transfers between devices: 13.9 us -> 12.5 us  [halving_reduce_scatter(): block = kept + lax.ppermute(sent, axis, stage_pairs(count, bit))]
    ppermute x8, waiting for transfers between devices: 14.2 us -> 12.8 us  [halving_reduce_scatter(): block = kept + lax.ppermute(sent, axis, stage_pairs(count, bit))]
  transfers between devices with their start and end apart: 24 -> 24, of which waited for: 11 -> 13; matrix products, arithmetic and copies ran while one was open for 19% -> 20% of each run, Pallas kernels for 0% -> 0%
where the time goes in v4:
time: 116 us; the launch traced here: 115 us
  starting transfers between devices  42 us (36%)
  other arithmetic  22.8 us (20%)
  waiting for transfers between devices  21 us (18%)
  local copies, waits for them, and re-layouts  18.1 us (16%)
  matrix products  8.28 us (7%)
  between operations  2.64 us (2%)
    ppermute x4, starting transfers between devices, with_halo(): lax.ppermute(lax.slice_in_dim(block, block.shape[dim] - width, None, axis...  14.5 us
    ppermute x8, waiting for transfers between devices, halving_reduce_scatter(): block = kept + lax.ppermute(sent, axis, stage_pairs(count, bit))  12.8 us
    ppermute x8, starting transfers between devices, halving_reduce_scatter(): block = kept + lax.ppermute(sent, axis, stage_pairs(count, bit))  12.5 us
    ppermute x8, starting transfers between devices, doubling_all_gather(): other = lax.ppermute(block, axis, stage_pairs(count, bit))  9.85 us
    reduce_sum x1, other arithmetic, forward_back(): centred = conv_out - jnp.mean(conv_out, axis=2, keepdims=True)  6.42 us
    ppermute x8, waiting for transfers between devices, doubling_all_gather(): other = lax.ppermute(block, axis, stage_pairs(count, bit))  5.88 us
    convert_element_type x1, other arithmetic, per_device(): running_input.astype(jnp.bfloat16)  5.72 us
    ppermute x4, starting transfers between devices, with_halo(): lax.ppermute(lax.slice_in_dim(block, 0, width, axis=dim), axis, backward)  5.16 us
  transfers between devices with their start and end apart: 24, of which 13 were waited for; matrix products, arithmetic and copies ran while one was open for 20% of the time, Pallas kernels for 0%

profile of v4, /device:TPU:0, one launch (start us, length us, event | category | flops | bytes accessed | tf_op | source)
XLA Modules:
  0.0 114.8 jit_solution(2662393390105772845)
XLA Ops:
  1.6 4.9 %collective-permute-start = (bf16[3,32,256]{2,1,0:T(8,128)(2,1)S(1)}, bf16[3,32,256]{2,1,0:T(8,128)(2,1)S(1)}, u32[]{:S(2)}, u32[]{:S(2)}) collective-permute-start(bf16[3,32,256]{2,1,0:T(8,128)(2,1)S(1)} %get-tuple-element.105), channel_id=1, source_target_pairs={{0,2},{2,4},{4,6},{6,8},{8,10},{10,12},{12,14},{1,3},{3,5},{5,7},{... | collective-permute-start | bytes 147464 | tf_op jit(solution)/shard_map/ppermute | solution.py:14
  6.5 1.3 %collective-permute-start.1 = (bf16[3,32,256]{2,1,0:T(8,128)(2,1)S(1)}, bf16[3,32,256]{2,1,0:T(8,128)(2,1)S(1)}, u32[]{:S(2)}, u32[]{:S(2)}) collective-permute-start(bf16[3,32,256]{2,1,0:T(8,128)(2,1)S(1)} %get-tuple-element.104), channel_id=1, source_target_pairs={{2,0},{4,2},{6,4},{8,6},{10,8},{12,10},{14,12},{3,1},{5,3},{7,5},{... | collective-permute-start | bytes 147464 | tf_op jit(solution)/shard_map/ppermute | solution.py:17
  11.3 1.6 %fusion.218 = (f32[1,256]{1,0:T(1,128)S(1)}, f32[1,256]{1,0:T(1,128)}, f32[1,256]{1,0:T(1,128)}, f32[1,256]{1,0:T(1,128)}, f32[1,256]{1,0:T(1,128)}, /*index=5*/...) fusion(f32[49,256]{1,0:T(8,128)} %param.13), kind=kLoop, calls=%fused_computation.513 | loop fusion | bytes 22528 | tf_op jit(solution)/shard_map/slice | solution.py:35
  14.0 1.5 %collective-permute-start.2 = (bf16[22,3,256]{2,1,0:T(4,128)(2,1)S(1)}, bf16[22,3,256]{2,1,0:T(4,128)(2,1)S(1)}, u32[]{:S(2)}, u32[]{:S(2)}) collective-permute-start(bf16[22,3,256]{2,1,0:T(4,128)(2,1)S(1)} %get-tuple-element.99), channel_id=1, source_target_pairs={{0,1},{2,3},{4,5},{6,7},{8,9},{10,11},{12,13},{14,15},{16,17},{18,... | collective-permute-start | bytes 101384 | tf_op jit(solution)/shard_map/ppermute | solution.py:14
  15.5 1.3 %collective-permute-start.3 = (bf16[22,3,256]{2,1,0:T(4,128)(2,1)S(1)}, bf16[22,3,256]{2,1,0:T(4,128)(2,1)S(1)}, u32[]{:S(2)}, u32[]{:S(2)}) collective-permute-start(bf16[22,3,256]{2,1,0:T(4,128)(2,1)S(1)} %get-tuple-element.100), channel_id=1, source_target_pairs={{1,0},{3,2},{5,4},{7,6},{9,8},{11,10},{13,12},{15,14},{17,16},{19,... | collective-permute-start | bytes 101384 | tf_op jit(solution)/shard_map/ppermute | solution.py:17
  18.6 6.4 %fusion.209 = (f32[16,32]{1,0:T(8,128)S(1)}, f32[16,32,256]{2,1,0:T(8,128)S(1)}) fusion(f32[256]{0:T(256)S(1)} %copy-done.99, f32[256]{0:T(256)} %bitcast.49, bf16[22,3,256]{2,1,0:T(4,128)(2,1)S(1)} %collective-permute-done.3, bf16[22,32,256]{2,1,0:T(8,128)(2,1)S(1)} %get-tuple-element.158, f32[256]{0:T(256)} %bitcast.48, f32[256]{0:T(256)S(1)} %bitcast.144, ...), kind=kLoop, calls=%fused_computation.505 | loop fusion | flops 35913216 | bytes 2840576 | tf_op jit(solution)/shard_map/reduce_sum | solution.py:56
  26.0 1.6 %multiply_convert_fusion = (bf16[512,1024]{1,0:T(8,128)(2,1)}, f32[512,1024]{1,0:T(8,128)S(1)}) fusion(f32[1024]{0:T(1024)S(1)} %copy-done.85, bf16[512,256]{1,0:T(8,128)(2,1)S(1)} %bitcast.140, bf16[256,1024]{1,0:T(8,128)(2,1)S(1)} %copy-done), kind=kOutput, calls=%fused_computation.48 | convolution fusion | flops 271581184 | bytes 3936256 | tf_op jit(solution)/shard_map/dot_general | solution.py:60
  28.9 1.5 %fusion.219 = f32[1024,256]{1,0:T(8,128)} fusion(bf16[512,1024]{1,0:T(8,128)(2,1)S(1)} %get-tuple-element.163, bf16[512,256]{1,0:T(8,128)(2,1)S(1)} %bitcast.141), kind=kOutput, calls=%fused_computation.514 | convolution fusion | flops 268435456 | bytes 2359296 | tf_op jit(solution)/shard_map/dot_general | solution.py:188
  31.7 1.7 %fusion.158 = (f32[256]{0:T(256)S(1)}, f32[256]{0:T(256)S(1)}, f32[256]{0:T(256)S(1)}, f32[256]{0:T(256)S(1)}, f32[256]{0:T(256)S(1)}, /*index=5*/f32[256]{0:T(2...) fusion(bf16[22,3,256]{2,1,0:T(4,128)(2,1)S(1)} %collective-permute-done.3, ...), kind=kLoop, calls=%fused_computation.314 | loop fusion | flops 7730944 | bytes 1983488 | tf_op jit(solution)/shard_map/reduce_sum | solution.py:204
  35.0 2.4 %fusion.220 = f32[1024,256]{1,0:T(8,128)} fusion(bf16[512,1024]{1,0:T(8,128)(2,1)S(1)} %copy-done.1, bf16[512,256]{1,0:T(8,128)(2,1)} %copy-done.6), kind=kOutput, calls=%fused_computation.515 | convolution fusion | flops 268435456 | bytes 2359296 | tf_op jit(solution)/shard_map/dot_general | solution.py:192
  37.9 2.1 %concatenate.137 = f32[1152,256]{1,0:T(8,128)S(1)} concatenate(f32[1024,256]{1,0:T(8,128)} %fusion.220, f32[4,256]{1,0:T(4,128)S(1)} %reshape.162, f32[1,256]{1,0:T(1,128)S(1)} %bitcast.223, f32[1,256]{1,0:T(1,128)S(1)} %bitcast.274, f32[2,256]{1,0:T(2,128)S(1)} %broadcast_in_dim.10, f32[120,256]{1,0:T(8,128)S(1)} %broadcast_in_dim.11), dimensions={0} | concatenate | bytes 2359296 | tf_op jit(solution)/shard_map/concatenate | solution.py:144
  41.2 5.0 %collective-permute-start.4 = (f32[3,32,256]{2,1,0:T(8,128)}, f32[3,32,256]{2,1,0:T(8,128)}, u32[]{:S(2)}, u32[]{:S(2)}) collective-permute-start(f32[3,32,256]{2,1,0:T(8,128)} %get-tuple-element.97), channel_id=1, source_target_pairs={{0,2},{2,4},{4,6},{6,8},{8,10},{10,12},{12,14},{1,3},{3,5},{5,7},{... | collective-permute-start | bytes 294920 | tf_op jit(solution)/shard_map/ppermute | solution.py:14
  49.9 2.8 %concatenate.136 = f32[1152,256]{1,0:T(8,128)S(1)} concatenate(f32[1024,256]{1,0:T(8,128)} %fusion.219, f32[49,256]{1,0:T(8,128)S(1)} %stack.199, f32[1,256]{1,0:T(1,128)} %bitcast.222, f32[1,256]{1,0:T(1,128)} %bitcast.221, f32[1,256]{1,0:T(1,128)S(1)} %bitcast.220, f32[4,256]{1,0:T(4,128)S(1)} %broadcast_in_dim.8, f32[72,256]{1,0:T(8,128)S(1)} %broadcast_in_dim.9), dimensions={0} | concatenate | bytes 2359296 | tf_op jit(solution)/shard_map/concatenate | solution.py:144
  54.5 1.3 %collective-permute-start.6 = (f32[22,3,256]{2,1,0:T(4,128)S(1)}, f32[22,3,256]{2,1,0:T(4,128)S(1)}, u32[]{:S(2)}, u32[]{:S(2)}) collective-permute-start(f32[22,3,256]{2,1,0:T(4,128)S(1)} %get-tuple-element.90), channel_id=1, source_target_pairs={{1,0},{3,2},{5,4},{7,6},{9,8},{11,10},{13,12},{15,14},{17,16},{19,... | collective-permute-start | bytes 202760 | tf_op jit(solution)/shard_map/ppermute | solution.py:17
  55.8 3.2 %collective-permute-start.7 = (f32[22,3,256]{2,1,0:T(4,128)S(1)}, f32[22,3,256]{2,1,0:T(4,128)S(1)}, u32[]{:S(2)}, u32[]{:S(2)}) collective-permute-start(f32[22,3,256]{2,1,0:T(4,128)S(1)} %get-tuple-element.91), channel_id=1, source_target_pairs={{0,1},{2,3},{4,5},{6,7},{8,9},{10,11},{12,13},{14,15},{16,17},{18,... | collective-permute-start | bytes 202760 | tf_op jit(solution)/shard_map/ppermute | solution.py:14
  61.3 5.7 %fusion.167 = bf16[16,32,256]{2,1,0:T(8,128)(2,1)} fusion(f32[22,35,256]{2,1,0:T(8,128)S(1)} %get-tuple-element.89, f32[16,32,256]{2,1,0:T(8,128)S(1)} %get-tuple-element.83, f32[3,32,256]{2,1,0:T(8,128)} %collective-permute-done.4, f32[22,35,256]{2,1,0:T(8,128)S(1)} %get-tuple-element.88, f32[3,32,256]{2,1,0:T(8,128)} %collective-permute-done.5, ...), kind=kLoop, calls=%fused_computation.375 | loop fusion | flops 13893632 | bytes 23315456 | tf_op jit(solution)/shard_map/convert_element_type | solution.py:237
  68.2 2.7 %collective-permute-start.17 = (f32[288,256]{1,0:T(8,128)S(1)}, f32[288,256]{1,0:T(8,128)S(1)}, u32[]{:S(2)}, u32[]{:S(2)}) collective-permute-start(f32[288,256]{1,0:T(8,128)S(1)} %constant_dynamic-slice_fusion.2), channel_id=1, source_target_pairs={{0,2},{2,0},{4,6},{6,4},{8,10},{10,8},{12,14},{14,12},{1,3},{3,1},... | collective-permute-start | bytes 884744 | tf_op jit(solution)/shard_map/ppermute | solution.py:117
  71.0 1.7 %collective-permute-start.9 = (f32[288,256]{1,0:T(8,128)S(1)}, f32[288,256]{1,0:T(8,128)S(1)}, u32[]{:S(2)}, u32[]{:S(2)}) collective-permute-start(f32[288,256]{1,0:T(8,128)S(1)} %constant_dynamic-slice_fusion.6), channel_id=1, source_target_pairs={{0,4},{2,6},{4,0},{6,2},{8,12},{10,14},{12,8},{14,10},{1,5},{3,7},... | collective-permute-start | bytes 884744 | tf_op jit(solution)/shard_map/ppermute | solution.py:117
  72.7 5.8 %collective-permute-done.17 = f32[288,256]{1,0:T(8,128)S(1)} collective-permute-done((f32[288,256]{1,0:T(8,128)S(1)}, f32[288,256]{1,0:T(8,128)S(1)}, u32[]{:S(2)}, u32[]{:S(2)}) %collective-permute-start.17) | collective-permute-done | bytes 294944 | tf_op jit(solution)/shard_map/ppermute | solution.py:117
  78.5 2.5 %collective-permute-start.18 = (f32[144,256]{1,0:T(8,128)S(1)}, f32[144,256]{1,0:T(8,128)S(1)}, u32[]{:S(2)}, u32[]{:S(2)}) collective-permute-start(f32[144,256]{1,0:T(8,128)S(1)} %constant_dynamic-slice_fusion.1), channel_id=1, source_target_pairs={{0,4},{2,6},{4,0},{6,2},{8,12},{10,14},{12,8},{14,10},{1,5},{3,7},... | collective-permute-start | bytes 442376 | tf_op jit(solution)/shard_map/ppermute | solution.py:117
  82.0 2.5 %collective-permute-done.18 = f32[144,256]{1,0:T(8,128)S(1)} collective-permute-done((f32[144,256]{1,0:T(8,128)S(1)}, f32[144,256]{1,0:T(8,128)S(1)}, u32[]{:S(2)}, u32[]{:S(2)}) %collective-permute-start.18) | collective-permute-done | bytes 147488 | tf_op jit(solution)/shard_map/ppermute | solution.py:117
  84.6 2.8 %collective-permute-start.19 = (f32[72,256]{1,0:T(8,128)S(1)}, f32[72,256]{1,0:T(8,128)S(1)}, u32[]{:S(2)}, u32[]{:S(2)}) collective-permute-start(f32[72,256]{1,0:T(8,128)S(1)} %constant_dynamic-slice_fusion), channel_id=1, source_target_pairs={{0,8},{2,10},{4,12},{6,14},{8,0},{10,2},{12,4},{14,6},{1,9},{3,11}... | collective-permute-start | bytes 221192 | tf_op jit(solution)/shard_map/ppermute | solution.py:117
  87.5 1.6 %collective-permute-start.11 = (f32[72,256]{1,0:T(8,128)S(1)}, f32[72,256]{1,0:T(8,128)S(1)}, u32[]{:S(2)}, u32[]{:S(2)}) collective-permute-start(f32[72,256]{1,0:T(8,128)S(1)} %constant_dynamic-slice_fusion.4), channel_id=1, source_target_pairs={{0,8},{2,10},{4,12},{6,14},{8,0},{10,2},{12,4},{14,6},{1,9},{3,11}... | collective-permute-start | bytes 221192 | tf_op jit(solution)/shard_map/ppermute | solution.py:117
  89.0 3.0 %collective-permute-done.19 = f32[72,256]{1,0:T(8,128)S(1)} collective-permute-done((f32[72,256]{1,0:T(8,128)S(1)}, f32[72,256]{1,0:T(8,128)S(1)}, u32[]{:S(2)}, u32[]{:S(2)}) %collective-permute-start.19) | collective-permute-done | bytes 73760 | tf_op jit(solution)/shard_map/ppermute | solution.py:117
  92.8 1.5 %collective-permute-done.11 = f32[72,256]{1,0:T(8,128)S(1)} collective-permute-done((f32[72,256]{1,0:T(8,128)S(1)}, f32[72,256]{1,0:T(8,128)S(1)}, u32[]{:S(2)}, u32[]{:S(2)}) %collective-permute-start.11) | collective-permute-done | bytes 73760 | tf_op jit(solution)/shard_map/ppermute | solution.py:117
  95.2 1.9 %collective-permute-done.20 = bf16[72,256]{1,0:T(8,128)(2,1)S(1)} collective-permute-done((bf16[72,256]{1,0:T(8,128)(2,1)S(1)}, bf16[72,256]{1,0:T(8,128)(2,1)S(1)}, u32[]{:S(2)}, u32[]{:S(2)}) %collective-permute-start.20) | collective-permute-done | bytes 36896 | tf_op jit(solution)/shard_map/ppermute | solution.py:124
  97.0 1.9 %collective-permute-start.21 = (bf16[144,256]{1,0:T(8,128)(2,1)S(1)}, bf16[144,256]{1,0:T(8,128)(2,1)S(1)}, u32[]{:S(2)}, u32[]{:S(2)}) collective-permute-start(bf16[144,256]{1,0:T(8,128)(2,1)S(1)} %constant_dynamic-update-slice_fusion.13), channel_id=1, source_target_pairs={{0,4},{2,6},{4,0},{6,2},{8,12},{10,14},{12,8},{14,10},{1,5},{3,7},... | collective-permute-start | bytes 221192 | tf_op jit(solution)/shard_map/ppermute | solution.py:124
  99.2 1.4 %collective-permute-start.13 = (bf16[144,256]{1,0:T(8,128)(2,1)S(1)}, bf16[144,256]{1,0:T(8,128)(2,1)S(1)}, u32[]{:S(2)}, u32[]{:S(2)}) collective-permute-start(bf16[144,256]{1,0:T(8,128)(2,1)S(1)} %constant_dynamic-update-slice_fusion.21), channel_id=1, source_target_pairs={{0,2},{2,0},{4,6},{6,4},{8,10},{10,8},{12,14},{14,12},{1,3},{3,1},... | collective-permute-start | bytes 221192 | tf_op jit(solution)/shard_map/ppermute | solution.py:124
  101.4 2.1 %collective-permute-start.22 = (bf16[288,256]{1,0:T(8,128)(2,1)S(1)}, bf16[288,256]{1,0:T(8,128)(2,1)S(1)}, u32[]{:S(2)}, u32[]{:S(2)}) collective-permute-start(bf16[288,256]{1,0:T(8,128)(2,1)S(1)} %constant_dynamic-update-slice_fusion.11), channel_id=1, source_target_pairs={{0,2},{2,0},{4,6},{6,4},{8,10},{10,8},{12,14},{14,12},{1,3},{3,1},... | collective-permute-start | bytes 442376 | tf_op jit(solution)/shard_map/ppermute | solution.py:124
  103.6 2.8 %collective-permute-start.14 = (bf16[288,256]{1,0:T(8,128)(2,1)S(1)}, bf16[288,256]{1,0:T(8,128)(2,1)S(1)}, u32[]{:S(2)}, u32[]{:S(2)}) collective-permute-start(bf16[288,256]{1,0:T(8,128)(2,1)S(1)} %constant_dynamic-update-slice_fusion.19), channel_id=1, source_target_pairs={{0,4},{2,6},{4,0},{6,2},{8,12},{10,14},{12,8},{14,10},{1,5},{3,7},... | collective-permute-start | bytes 442376 | tf_op jit(solution)/shard_map/ppermute | solution.py:124
  106.7 2.8 %collective-permute-done.14 = bf16[288,256]{1,0:T(8,128)(2,1)S(1)} collective-permute-done((bf16[288,256]{1,0:T(8,128)(2,1)S(1)}, bf16[288,256]{1,0:T(8,128)(2,1)S(1)}, u32[]{:S(2)}, u32[]{:S(2)}) %collective-permute-start.14) | collective-permute-done | bytes 147488 | tf_op jit(solution)/shard_map/ppermute | solution.py:124
  113.5 1.3 %copy.21 = f32[256,1024]{1,0:T(8,128)} copy(f32[256,1024]{0,1:T(8,128)S(1)} %slice_bitcast_fusion) | data formatting | bytes 2097152
  (315 shorter events, 29.9 us)
Async XLA Ops:
  0.6 25.3 %copy-start = (bf16[256,1024]{1,0:T(8,128)(2,1)S(1)}, bf16[256,1024]{1,0:T(8,128)(2,1)}, u32[]{:S(2)}) copy-start(bf16[256,1024]{1,0:T(8,128)(2,1)} %param.17) | copy-start | bytes 1572868
  0.7 17.9 %copy-start.2 = (bf16[16,32,256]{2,1,0:T(8,128)(2,1)S(1)}, bf16[16,32,256]{2,1,0:T(8,128)(2,1)}, u32[]{:S(2)}) copy-start(bf16[16,32,256]{2,1,0:T(8,128)(2,1)} %param.11) | copy-start | bytes 786436
  0.7 17.9 %copy-start.99 = (f32[256]{0:T(256)S(1)}, f32[256]{0:T(256)}, u32[]{:S(2)}) copy-start(f32[256]{0:T(256)} %param.14) | copy-start | bytes 3076
  1.6 11.2 %collective-permute-start = (bf16[3,32,256]{2,1,0:T(8,128)(2,1)S(1)}, bf16[3,32,256]{2,1,0:T(8,128)(2,1)S(1)}, u32[]{:S(2)}, u32[]{:S(2)}) collective-permute-start(bf16[3,32,256]{2,1,0:T(8,128)(2,1)S(1)} %get-tuple-element.105), channel_id=1, source_target_pairs={{0,2},{2,4},{4,6},{6,8},{8,10},{10,12},{12,14},{1,3},{3,5},{5,7},{... | collective-permute-start | bytes 147464 | tf_op jit(solution)/shard_map/ppermute | solution.py:14
  6.5 7.4 %collective-permute-start.1 = (bf16[3,32,256]{2,1,0:T(8,128)(2,1)S(1)}, bf16[3,32,256]{2,1,0:T(8,128)(2,1)S(1)}, u32[]{:S(2)}, u32[]{:S(2)}) collective-permute-start(bf16[3,32,256]{2,1,0:T(8,128)(2,1)S(1)} %get-tuple-element.104), channel_id=1, source_target_pairs={{2,0},{4,2},{6,4},{8,6},{10,8},{12,10},{14,12},{3,1},{5,3},{7,5},{... | collective-permute-start | bytes 147464 | tf_op jit(solution)/shard_map/ppermute | solution.py:17
  8.9 16.2 %copy-start.10 = (f32[1,256]{1,0:T(1,128)}, f32[1,256]{1,0:T(1,128)S(1)}, u32[]{:S(2)}) copy-start(f32[1,256]{1,0:T(1,128)S(1)} %get-tuple-element.108) | copy-start | bytes 3076
  8.9 16.2 %copy-start.12 = (f32[1,256]{1,0:T(1,128)}, f32[1,256]{1,0:T(1,128)S(1)}, u32[]{:S(2)}) copy-start(f32[1,256]{1,0:T(1,128)S(1)} %get-tuple-element.109) | copy-start | bytes 3076
  8.9 16.2 %copy-start.14 = (f32[1,256]{1,0:T(1,128)}, f32[1,256]{1,0:T(1,128)S(1)}, u32[]{:S(2)}) copy-start(f32[1,256]{1,0:T(1,128)S(1)} %get-tuple-element.110) | copy-start | bytes 3076
  8.9 16.2 %copy-start.16 = (f32[1,256]{1,0:T(1,128)}, f32[1,256]{1,0:T(1,128)S(1)}, u32[]{:S(2)}) copy-start(f32[1,256]{1,0:T(1,128)S(1)} %get-tuple-element.111) | copy-start | bytes 3076
  11.3 16.3 %copy-start.6 = (bf16[512,256]{1,0:T(8,128)(2,1)}, bf16[512,256]{1,0:T(8,128)(2,1)S(1)}, u32[]{:S(2)}) copy-start(bf16[512,256]{1,0:T(8,128)(2,1)S(1)} %fusion.165) | copy-start | bytes 786436
  14.0 3.5 %collective-permute-start.2 = (bf16[22,3,256]{2,1,0:T(4,128)(2,1)S(1)}, bf16[22,3,256]{2,1,0:T(4,128)(2,1)S(1)}, u32[]{:S(2)}, u32[]{:S(2)}) collective-permute-start(bf16[22,3,256]{2,1,0:T(4,128)(2,1)S(1)} %get-tuple-element.99), channel_id=1, source_target_pairs={{0,1},{2,3},{4,5},{6,7},{8,9},{10,11},{12,13},{14,15},{16,17},{18,... | collective-permute-start | bytes 101384 | tf_op jit(solution)/shard_map/ppermute | solution.py:14
  15.5 3.1 %collective-permute-start.3 = (bf16[22,3,256]{2,1,0:T(4,128)(2,1)S(1)}, bf16[22,3,256]{2,1,0:T(4,128)(2,1)S(1)}, u32[]{:S(2)}, u32[]{:S(2)}) collective-permute-start(bf16[22,3,256]{2,1,0:T(4,128)(2,1)S(1)} %get-tuple-element.100), channel_id=1, source_target_pairs={{1,0},{3,2},{5,4},{7,6},{9,8},{11,10},{13,12},{15,14},{17,16},{19,... | collective-permute-start | bytes 101384 | tf_op jit(solution)/shard_map/ppermute | solution.py:17
  41.0 26.0 %collective-permute-start.16 = (f32[576,256]{1,0:T(8,128)}, f32[576,256]{1,0:T(8,128)}, u32[]{:S(2)}, u32[]{:S(2)}) collective-permute-start(f32[576,256]{1,0:T(8,128)} %constant_dynamic-slice_fusion.3), channel_id=1, source_target_pairs={{0,1},{1,0},{2,3},{3,2},{4,5},{5,4},{6,7},{7,6},{8,9},{9,8},{10,11... | collective-permute-start | bytes 1769480 | tf_op jit(solution)/shard_map/ppermute | solution.py:117
  41.2 11.5 %collective-permute-start.4 = (f32[3,32,256]{2,1,0:T(8,128)}, f32[3,32,256]{2,1,0:T(8,128)}, u32[]{:S(2)}, u32[]{:S(2)}) collective-permute-start(f32[3,32,256]{2,1,0:T(8,128)} %get-tuple-element.97), channel_id=1, source_target_pairs={{0,2},{2,4},{4,6},{6,8},{8,10},{10,12},{12,14},{1,3},{3,5},{5,7},{... | collective-permute-start | bytes 294920 | tf_op jit(solution)/shard_map/ppermute | solution.py:14
  46.2 7.1 %collective-permute-start.5 = (f32[3,32,256]{2,1,0:T(8,128)}, f32[3,32,256]{2,1,0:T(8,128)}, u32[]{:S(2)}, u32[]{:S(2)}) collective-permute-start(f32[3,32,256]{2,1,0:T(8,128)} %get-tuple-element.98), channel_id=1, source_target_pairs={{2,0},{4,2},{6,4},{8,6},{10,8},{12,10},{14,12},{3,1},{5,3},{7,5},{... | collective-permute-start | bytes 294920 | tf_op jit(solution)/shard_map/ppermute | solution.py:17
  54.5 4.7 %collective-permute-start.6 = (f32[22,3,256]{2,1,0:T(4,128)S(1)}, f32[22,3,256]{2,1,0:T(4,128)S(1)}, u32[]{:S(2)}, u32[]{:S(2)}) collective-permute-start(f32[22,3,256]{2,1,0:T(4,128)S(1)} %get-tuple-element.90), channel_id=1, source_target_pairs={{1,0},{3,2},{5,4},{7,6},{9,8},{11,10},{13,12},{15,14},{17,16},{19,... | collective-permute-start | bytes 202760 | tf_op jit(solution)/shard_map/ppermute | solution.py:17
  55.8 4.0 %collective-permute-start.7 = (f32[22,3,256]{2,1,0:T(4,128)S(1)}, f32[22,3,256]{2,1,0:T(4,128)S(1)}, u32[]{:S(2)}, u32[]{:S(2)}) collective-permute-start(f32[22,3,256]{2,1,0:T(4,128)S(1)} %get-tuple-element.91), channel_id=1, source_target_pairs={{0,1},{2,3},{4,5},{6,7},{8,9},{10,11},{12,13},{14,15},{16,17},{18,... | collective-permute-start | bytes 202760 | tf_op jit(solution)/shard_map/ppermute | solution.py:14
  59.1 11.8 %collective-permute-start.8 = (f32[576,256]{1,0:T(8,128)S(1)}, f32[576,256]{1,0:T(8,128)S(1)}, u32[]{:S(2)}, u32[]{:S(2)}) collective-permute-start(f32[576,256]{1,0:T(8,128)S(1)} %constant_dynamic-slice_fusion.7), channel_id=1, source_target_pairs={{0,1},{1,0},{2,3},{3,2},{4,5},{5,4},{6,7},{7,6},{8,9},{9,8},{10,11... | collective-permute-start | bytes 1769480 | tf_op jit(solution)/shard_map/ppermute | solution.py:117
  68.2 10.2 %collective-permute-start.17 = (f32[288,256]{1,0:T(8,128)S(1)}, f32[288,256]{1,0:T(8,128)S(1)}, u32[]{:S(2)}, u32[]{:S(2)}) collective-permute-start(f32[288,256]{1,0:T(8,128)S(1)} %constant_dynamic-slice_fusion.2), channel_id=1, source_target_pairs={{0,2},{2,0},{4,6},{6,4},{8,10},{10,8},{12,14},{14,12},{1,3},{3,1},... | collective-permute-start | bytes 884744 | tf_op jit(solution)/shard_map/ppermute | solution.py:117
  71.0 10.0 %collective-permute-start.9 = (f32[288,256]{1,0:T(8,128)S(1)}, f32[288,256]{1,0:T(8,128)S(1)}, u32[]{:S(2)}, u32[]{:S(2)}) collective-permute-start(f32[288,256]{1,0:T(8,128)S(1)} %constant_dynamic-slice_fusion.6), channel_id=1, source_target_pairs={{0,4},{2,6},{4,0},{6,2},{8,12},{10,14},{12,8},{14,10},{1,5},{3,7},... | collective-permute-start | bytes 884744 | tf_op jit(solution)/shard_map/ppermute | solution.py:117
  78.5 6.1 %collective-permute-start.18 = (f32[144,256]{1,0:T(8,128)S(1)}, f32[144,256]{1,0:T(8,128)S(1)}, u32[]{:S(2)}, u32[]{:S(2)}) collective-permute-start(f32[144,256]{1,0:T(8,128)S(1)} %constant_dynamic-slice_fusion.1), channel_id=1, source_target_pairs={{0,4},{2,6},{4,0},{6,2},{8,12},{10,14},{12,8},{14,10},{1,5},{3,7},... | collective-permute-start | bytes 442376 | tf_op jit(solution)/shard_map/ppermute | solution.py:117
  81.1 6.3 %collective-permute-start.10 = (f32[144,256]{1,0:T(8,128)S(1)}, f32[144,256]{1,0:T(8,128)S(1)}, u32[]{:S(2)}, u32[]{:S(2)}) collective-permute-start(f32[144,256]{1,0:T(8,128)S(1)} %constant_dynamic-slice_fusion.5), channel_id=1, source_target_pairs={{0,2},{2,0},{4,6},{6,4},{8,10},{10,8},{12,14},{14,12},{1,3},{3,1},... | collective-permute-start | bytes 442376 | tf_op jit(solution)/shard_map/ppermute | solution.py:117
  84.6 7.4 %collective-permute-start.19 = (f32[72,256]{1,0:T(8,128)S(1)}, f32[72,256]{1,0:T(8,128)S(1)}, u32[]{:S(2)}, u32[]{:S(2)}) collective-permute-start(f32[72,256]{1,0:T(8,128)S(1)} %constant_dynamic-slice_fusion), channel_id=1, source_target_pairs={{0,8},{2,10},{4,12},{6,14},{8,0},{10,2},{12,4},{14,6},{1,9},{3,11}... | collective-permute-start | bytes 221192 | tf_op jit(solution)/shard_map/ppermute | solution.py:117
  87.5 6.8 %collective-permute-start.11 = (f32[72,256]{1,0:T(8,128)S(1)}, f32[72,256]{1,0:T(8,128)S(1)}, u32[]{:S(2)}, u32[]{:S(2)}) collective-permute-start(f32[72,256]{1,0:T(8,128)S(1)} %constant_dynamic-slice_fusion.4), channel_id=1, source_target_pairs={{0,8},{2,10},{4,12},{6,14},{8,0},{10,2},{12,4},{14,6},{1,9},{3,11}... | collective-permute-start | bytes 221192 | tf_op jit(solution)/shard_map/ppermute | solution.py:117
  92.1 5.0 %collective-permute-start.20 = (bf16[72,256]{1,0:T(8,128)(2,1)S(1)}, bf16[72,256]{1,0:T(8,128)(2,1)S(1)}, u32[]{:S(2)}, u32[]{:S(2)}) collective-permute-start(bf16[72,256]{1,0:T(8,128)(2,1)S(1)} %get-tuple-element.80), channel_id=1, source_target_pairs={{0,8},{2,10},{4,12},{6,14},{8,0},{10,2},{12,4},{14,6},{1,9},{3,11}... | collective-permute-start | bytes 110600 | tf_op jit(solution)/shard_map/ppermute | solution.py:124
  94.3 4.9 %collective-permute-start.12 = (bf16[72,256]{1,0:T(8,128)(2,1)S(1)}, bf16[72,256]{1,0:T(8,128)(2,1)S(1)}, u32[]{:S(2)}, u32[]{:S(2)}) collective-permute-start(bf16[72,256]{1,0:T(8,128)(2,1)S(1)} %get-tuple-element.82), channel_id=1, source_target_pairs={{0,8},{2,10},{4,12},{6,14},{8,0},{10,2},{12,4},{14,6},{1,9},{3,11}... | collective-permute-start | bytes 110600 | tf_op jit(solution)/shard_map/ppermute | solution.py:124
  97.0 4.4 %collective-permute-start.21 = (bf16[144,256]{1,0:T(8,128)(2,1)S(1)}, bf16[144,256]{1,0:T(8,128)(2,1)S(1)}, u32[]{:S(2)}, u32[]{:S(2)}) collective-permute-start(bf16[144,256]{1,0:T(8,128)(2,1)S(1)} %constant_dynamic-update-slice_fusion.13), channel_id=1, source_target_pairs={{0,4},{2,6},{4,0},{6,2},{8,12},{10,14},{12,8},{14,10},{1,5},{3,7},... | collective-permute-start | bytes 221192 | tf_op jit(solution)/shard_map/ppermute | solution.py:124
  99.2 4.4 %collective-permute-start.13 = (bf16[144,256]{1,0:T(8,128)(2,1)S(1)}, bf16[144,256]{1,0:T(8,128)(2,1)S(1)}, u32[]{:S(2)}, u32[]{:S(2)}) collective-permute-start(bf16[144,256]{1,0:T(8,128)(2,1)S(1)} %constant_dynamic-update-slice_fusion.21), channel_id=1, source_target_pairs={{0,2},{2,0},{4,6},{6,4},{8,10},{10,8},{12,14},{14,12},{1,3},{3,1},... | collective-permute-start | bytes 221192 | tf_op jit(solution)/shard_map/ppermute | solution.py:124
  101.4 5.2 %collective-permute-start.22 = (bf16[288,256]{1,0:T(8,128)(2,1)S(1)}, bf16[288,256]{1,0:T(8,128)(2,1)S(1)}, u32[]{:S(2)}, u32[]{:S(2)}) collective-permute-start(bf16[288,256]{1,0:T(8,128)(2,1)S(1)} %constant_dynamic-update-slice_fusion.11), channel_id=1, source_target_pairs={{0,2},{2,0},{4,6},{6,4},{8,10},{10,8},{12,14},{14,12},{1,3},{3,1},... | collective-permute-start | bytes 442376 | tf_op jit(solution)/shard_map/ppermute | solution.py:124
  103.6 5.9 %collective-permute-start.14 = (bf16[288,256]{1,0:T(8,128)(2,1)S(1)}, bf16[288,256]{1,0:T(8,128)(2,1)S(1)}, u32[]{:S(2)}, u32[]{:S(2)}) collective-permute-start(bf16[288,256]{1,0:T(8,128)(2,1)S(1)} %constant_dynamic-update-slice_fusion.19), channel_id=1, source_target_pairs={{0,4},{2,6},{4,0},{6,2},{8,12},{10,14},{12,8},{14,10},{1,5},{3,7},... | collective-permute-start | bytes 442376 | tf_op jit(solution)/shard_map/ppermute | solution.py:124
  106.6 3.1 %collective-permute-start.23 = (bf16[576,256]{1,0:T(8,128)(2,1)S(1)}, bf16[576,256]{1,0:T(8,128)(2,1)S(1)}, u32[]{:S(2)}, u32[]{:S(2)}) collective-permute-start(bf16[576,256]{1,0:T(8,128)(2,1)S(1)} %constant_dynamic-update-slice_fusion.9), channel_id=1, source_target_pairs={{0,1},{1,0},{2,3},{3,2},{4,5},{5,4},{6,7},{7,6},{8,9},{9,8},{10,11... | collective-permute-start | bytes 884744 | tf_op jit(solution)/shard_map/ppermute | solution.py:124
  109.5 2.0 %collective-permute-start.15 = (bf16[576,256]{1,0:T(8,128)(2,1)S(1)}, bf16[576,256]{1,0:T(8,128)(2,1)S(1)}, u32[]{:S(2)}, u32[]{:S(2)}) collective-permute-start(bf16[576,256]{1,0:T(8,128)(2,1)S(1)} %constant_dynamic-update-slice_fusion.17), channel_id=1, source_target_pairs={{0,1},{1,0},{2,3},{3,2},{4,5},{5,4},{6,7},{7,6},{8,9},{9,8},{10,11... | collective-permute-start | bytes 884744 | tf_op jit(solution)/shard_map/ppermute | solution.py:124
  (96 other events, 977.0 us)
